TPU v7x, 512 devices: a whole 4x8x8 slice. The times are simulated.
512 devices in a mesh: op: 16 (over y_lo, z), bond: 32 (over y_hi, x, core).
Axes of the slice: x: 4, y: 8 (y_hi: 4, y_lo: 2; y = y_hi * 2 + y_lo), z: 8, core: 2. Of those that a mesh axis runs over, the one named last changes fastest.
Arguments:
- vectors: bfloat16 [2, 64, 256, 256], P(None, 'bond'), may hold values from -6 to 6
- left_ops: bfloat16 [128, 64, 256, 256], P('op', 'bond'), may hold values from -0.03125 to 0.03125
- right_ops: bfloat16 [128, 64, 256, 256], P('op', 'bond'), may hold values from -0.375 to 0.375
- block_sizes: int32 [64, 2], P('bond'), may hold values from 32 to 256, as said below
- term_shifts: int32 [128], P('op'), may hold values from -1 to 1
Outputs:
- sigma: float32 [2, 64, 256, 256], P(None, 'bond', 'op')
Inputs may be any that keep to these rules, and one draw needn't show every extreme that they name: `block_sizes`: some block has both live dimensions 256 and some other block both 256 // 8.
All inputs are finite; a program needn't handle non-finite values.
Results may differ from a plain program's by a relative error of at most 0.0029.
Values may be sent and summed in bfloat16 or wider, within the bound.
No kernel may reach another device: no remote copies, remote signals or barrier semaphores. Data moves between devices by JAX's collectives and lax.ppermute only.
A program may use at most 64 MiB of HBM per device.

v0:
```python
import jax
import jax.numpy as jnp
from jax import lax
from jax.sharding import PartitionSpec as P


def extended(cells, sides, width):
    for axis, dim in sides:
        count = lax.axis_size(axis)
        ends = count - 1
        head = lax.slice_in_dim(cells, 0, width, axis=dim)
        tail = lax.slice_in_dim(cells, cells.shape[dim] - width, cells.shape[dim], axis=dim)
        cells = jnp.concatenate(
            [
                lax.ppermute(tail, axis, [(i, (i + 1) % count) for i in range(ends)]),
                cells,
                lax.ppermute(head, axis, [((i + 1) % count, i) for i in range(ends)]),
            ],
            axis=dim,
        )
    return cells


def per_device(vectors, left_ops, right_ops, block_sizes, term_shifts):
    block_count = vectors.shape[1]
    block_order = vectors.shape[2]
    row_index = jnp.arange(block_order, dtype=jnp.int32)
    live_mask = (row_index[None, :, None] < block_sizes[:, 0][:, None, None]) & (
        row_index[None, None, :] < block_sizes[:, 1][:, None, None]
    )
    masked = jnp.where(live_mask[None], vectors, jnp.zeros((), vectors.dtype))
    padded = extended(masked, (("bond", 1),), 1)

    def add_term(accumulated, operands):
        left_block, right_block, term_shift = operands
        start_block = 1 - term_shift
        source_blocks = lax.dynamic_slice_in_dim(padded, start_block, block_count, 1)
        half_product = jnp.einsum(
            "bik,vbkj->vbij", left_block, source_blocks, preferred_element_type=jnp.float32
        ).astype(jnp.bfloat16)
        term_value = jnp.einsum(
            "vbij,blj->vbil", half_product, right_block, preferred_element_type=jnp.float32
        )
        return (accumulated + term_value, None)

    initial = jnp.zeros((vectors.shape[0], block_count, block_order, block_order), jnp.float32)
    accumulated, _ = lax.scan(add_term, initial, (left_ops, right_ops, term_shifts))
    op_count = lax.axis_size("op")
    share_rows = block_order // op_count
    first_row = lax.axis_index("op") * share_rows
    summed = lax.psum(accumulated, "op")
    own_share = lax.dynamic_slice_in_dim(summed, first_row, share_rows, 2)
    live_share = lax.dynamic_slice_in_dim(live_mask, first_row, share_rows, 1)
    return jnp.where(live_share[None], own_share, jnp.zeros((), own_share.dtype))


def solution(mesh):
    in_specs = (
        P(None, "bond", None, None),
        P("op", "bond", None, None),
        P("op", "bond", None, None),
        P("bond", None),
        P("op"),
    )
    out_specs = P(None, "bond", "op", None)
    return jax.shard_map(
        per_device, mesh=mesh, in_specs=in_specs, out_specs=out_specs, check_vma=False
    )
```

profile of v0, /device:TPU:2, one launch (start us, length us, event | category | flops | bytes accessed | tf_op | source)
XLA Modules:
  0.0 213.6 jit_solution(7319213809346613324)
XLA Ops:
  6.5 0.0 all-reduce.2.cloned.1.call-start
  6.5 1.0 slice_reduce_fusion.1
  7.5 0.1 iota_compare_fusion
  7.6 0.1 broadcast_and_fusion
  7.7 0.0 copy-start
  7.7 1.1 broadcast_select_fusion
  8.9 1.9 collective-permute-start
  10.8 3.6 %collective-permute-start.1 = (bf16[2,1,256,256]{3,2,1,0:T(8,128)(2,1)S(1)}, bf16[2,1,256,256]{3,2,1,0:T(8,128)(2,1)S(1)}, u32[]{:S(2)}, u32[]{:S(2)}) collective-permute-start(bf16[2,1,256,256]{3,2,1,0:T(8,128)(2,1)S(1)} %get-tuple-element.119), channel_id=1, source_target_pairs={{1,0},{2,1},{3,2},{4,3},{5,4},{6,5},{7,6},{8,7},{9,8},{10,9},{11,1... | collective-permute-start | bytes 786440 | tf_op jit(solution)/shard_map/ppermute | solution.py:17
  14.5 2.1 collective-permute-done
  16.6 1.8 collective-permute-done.1
  18.3 0.1 pad_maximum_fusion
  18.5 0.0 copy-done
  18.5 29.0 %while.13 = (s32[]{:T(128)}, f32[2,2,256,256]{2,3,0,1:T(8,128)S(1)}, bf16[8,2,256,256]{3,2,1,0:T(8,128)(2,1)}, s32[8]{0:T(128)S(1)}, bf16[2,4,256,256]{3,2,1,0:T...) while((s32[]{:T(128)}, ...), condition=%wide.region_1.2_spmd.clone, body=%wide.region_0.1_spmd.clone.sunk | while | flops 269221888 | bytes 3147952 | solution.py:47
  18.5 0.7 dynamic_slice.60
  20.4 1.7 fusion.20
  22.1 0.7 dynamic_slice.60
  24.0 1.7 fusion.20
  25.7 0.7 dynamic_slice.60
  27.7 1.7 fusion.20
  29.4 0.7 dynamic_slice.60
  31.3 1.7 fusion.20
  33.0 0.7 dynamic_slice.60
  34.9 1.7 fusion.20
  36.6 0.7 dynamic_slice.60
  38.5 1.7 fusion.20
  40.2 0.7 dynamic_slice.60
  42.2 1.7 fusion.20
  43.9 0.7 dynamic_slice.60
  45.8 1.7 fusion.20
  47.5 1.4 copy.6
  48.9 0.0 all-reduce.2.cloned.1.call-update
  48.9 156.4 %all-reduce.2.cloned.1.call-done = f32[2,2,256,256]{3,2,1,0:T(8,128)} async-done(((f32[2,2,256,256]{3,2,1,0:T(8,128)}), f32[2,2,256,256]{3,2,1,0:T(8,128)}) %all-reduce.2.cloned.1.call-update) | async-done | bytes 1048592 | tf_op jit(solution)/shard_map/psum | solution.py:51
  205.3 1.5 dynamic-slice_select_fusion
  (3 shorter events, 0.0 us)
Async XLA Ops:
  6.5 198.7 %all-reduce.2.cloned.1.call-start = ((), (), s32[]{:S(2)}) async-start(), calls=%async_computation | async-start | bytes 2097152 | tf_op jit(solution)/shard_map/psum | solution.py:51
  7.7 10.7 %copy-start = (s32[8]{0:T(128)S(1)}, s32[8]{0:T(128)}, u32[]{:S(2)}) copy-start(s32[8]{0:T(128)} %param.11) | copy-start | bytes 100
  8.9 7.7 %collective-permute-start = (bf16[2,1,256,256]{3,2,1,0:T(8,128)(2,1)S(1)}, bf16[2,1,256,256]{3,2,1,0:T(8,128)(2,1)S(1)}, u32[]{:S(2)}, u32[]{:S(2)}) collective-permute-start(bf16[2,1,256,256]{3,2,1,0:T(8,128)(2,1)S(1)} %get-tuple-element.118), channel_id=1, source_target_pairs={{0,1},{1,2},{2,3},{3,4},{4,5},{5,6},{6,7},{7,8},{8,9},{9,10},{10,1... | collective-permute-start | bytes 786440 | tf_op jit(solution)/shard_map/ppermute | solution.py:15
  10.8 7.5 %collective-permute-start.1 = (bf16[2,1,256,256]{3,2,1,0:T(8,128)(2,1)S(1)}, bf16[2,1,256,256]{3,2,1,0:T(8,128)(2,1)S(1)}, u32[]{:S(2)}, u32[]{:S(2)}) collective-permute-start(bf16[2,1,256,256]{3,2,1,0:T(8,128)(2,1)S(1)} %get-tuple-element.119), channel_id=1, source_target_pairs={{1,0},{2,1},{3,2},{4,3},{5,4},{6,5},{7,6},{8,7},{9,8},{10,9},{11,1... | collective-permute-start | bytes 786440 | tf_op jit(solution)/shard_map/ppermute | solution.py:17
Sparse Core Ops, SparseCore 0:
  49.0 156.2 all-reduce.1
where the time goes:
time: 214 us
  waiting for transfers between devices  160 us (75%)
  between operations  13.5 us (6%)
  matrix products  13.4 us (6%)
  loops' own time  10.4 us (5%)
  local copies, waits for them, and re-layouts  7.58 us (4%)
  starting transfers between devices  5.56 us (3%)
  other arithmetic  2.93 us (1%)
    psum x1, waiting for transfers between devices, per_device(): summed = lax.psum(accumulated, 'op')  156 us
    dot_general x8, matrix products, add_term(): jnp.einsum('vbij,blj->vbil', half_product, right_block, preferred_element...  13.4 us
    another operation x1, loops' own time, per_device(): lax.scan(add_term, initial, (left_ops, right_ops, term_shifts))  10.4 us
    dynamic_slice x8, local copies, waits for them, and re-layouts, per_device(): lax.scan(add_term, initial, (left_ops, right_ops, term_shifts))  5.2 us
  transfers between devices with their start and end apart: 3, of which 3 were waited for; matrix products, arithmetic and copies ran while one was open for 0% of the time, Pallas kernels for 0%

commit v1 on v0

v1 whole, which is shorter than its diff:
```python
import jax
import jax.numpy as jnp
from jax import lax
from jax.sharding import PartitionSpec as P


def extended(cells, axis, dim):
    count = lax.axis_size(axis)
    ends = count - 1
    head = lax.slice_in_dim(cells, 0, 1, axis=dim)
    tail = lax.slice_in_dim(cells, cells.shape[dim] - 1, cells.shape[dim], axis=dim)
    return jnp.concatenate(
        [
            lax.ppermute(tail, axis, [(i, (i + 1) % count) for i in range(ends)]),
            cells,
            lax.ppermute(head, axis, [((i + 1) % count, i) for i in range(ends)]),
        ],
        axis=dim,
    )


def per_device(vectors, left_ops, right_ops, block_sizes, term_shifts):
    block_count = vectors.shape[1]
    block_order = vectors.shape[2]
    row_index = jnp.arange(block_order, dtype=jnp.int32)
    live_mask = (row_index[None, :, None] < block_sizes[:, 0][:, None, None]) & (
        row_index[None, None, :] < block_sizes[:, 1][:, None, None]
    )
    masked = jnp.where(live_mask[None], vectors, jnp.zeros((), vectors.dtype))
    padded = extended(masked, "bond", 1)

    shift = term_shifts[:, None, None, None, None]
    sources = jnp.where(
        shift == 1,
        padded[None, :, 0:block_count],
        jnp.where(shift == 0, padded[None, :, 1 : block_count + 1], padded[None, :, 2 : block_count + 2]),
    )
    half = jnp.einsum(
        "tbik,tvbkj->tvbij", left_ops, sources, preferred_element_type=jnp.float32
    ).astype(jnp.bfloat16)
    partial = jnp.einsum("tvbij,tblj->vbil", half, right_ops, preferred_element_type=jnp.float32)

    op_count = lax.axis_size("op")
    share_rows = block_order // op_count
    shares = partial.reshape(partial.shape[0], block_count, op_count, share_rows, block_order)
    received = lax.all_to_all(shares, "op", 2, 2, tiled=False)
    own_share = received.sum(axis=2)
    first_row = lax.axis_index("op") * share_rows
    live_share = lax.dynamic_slice_in_dim(live_mask, first_row, share_rows, 1)
    return jnp.where(live_share[None], own_share, jnp.zeros((), own_share.dtype))


def solution(mesh):
    in_specs = (
        P(None, "bond", None, None),
        P("op", "bond", None, None),
        P("op", "bond", None, None),
        P("bond", None),
        P("op"),
    )
    out_specs = P(None, "bond", "op", None)
    return jax.shard_map(
        per_device, mesh=mesh, in_specs=in_specs, out_specs=out_specs, check_vma=False
    )
```

time: 214 us -> 62.7 us (0.29)
  the two profiles are of different devices: /device:TPU:2 before, /device:TPU:29 now
where the time goes in v1:
time: 62.7 us; the launch traced here: 62.3 us
  waiting for transfers between devices  33.9 us (54%)
  starting transfers between devices  16.5 us (26%)
  matrix products  5.48 us (9%)
  local copies, waits for them, and re-layouts  4.09 us (7%)
  other arithmetic  2.3 us (4%)
    all_to_all x1, waiting for transfers between devices, per_device(): received = lax.all_to_all(shares, 'op', 2, 2, tiled=False)  28.1 us
    all_to_all x1, starting transfers between devices, per_device(): received = lax.all_to_all(shares, 'op', 2, 2, tiled=False)  11.2 us
    dot_general x1, matrix products, per_device(): jnp.einsum('tvbij,tblj->vbil', half, right_ops, preferred_element_type=jn...  5.48 us
    ppermute x1, waiting for transfers between devices, extended(): lax.ppermute(head, axis, [((i + 1) % count, i) for i in range(ends)])  4.4 us
    ppermute x1, starting transfers between devices, extended(): lax.ppermute(tail, axis, [(i, (i + 1) % count) for i in range(ends)])  3.39 us
    reshape x1, local copies, waits for them, and re-layouts, per_device(): partial.reshape(partial.shape[0], block_count, op_count, share_rows, bloc...  2.34 us
    ppermute x1, starting transfers between devices, extended(): lax.ppermute(head, axis, [((i + 1) % count, i) for i in range(ends)])  1.92 us
    ppermute x1, waiting for transfers between devices, extended(): lax.ppermute(tail, axis, [(i, (i + 1) % count) for i in range(ends)])  1.34 us
  transfers between devices with their start and end apart: 3, of which 3 were waited for; matrix products, arithmetic and copies ran while one was open for 0% of the time, Pallas kernels for 0%

profile of v1, /device:TPU:29, one launch (start us, length us, event | category | flops | bytes accessed | tf_op | source)
XLA Modules:
  0.0 62.3 jit_solution(10075210610561927438)
XLA Ops:
  0.0 0.0 copy-start
  0.0 0.0 copy-start.1
  0.0 1.1 %slice_reduce_fusion.1 = (s32[2]{0:T(128)S(1)}, s32[2]{0:T(128)S(1)}) fusion(s32[2,2]{1,0:T(2,128)} %param.8), kind=kLoop, calls=%fused_computation.16 | loop fusion | bytes 32 | tf_op jit(solution)/shard_map/slice | solution.py:26
  1.1 0.1 iota_compare_fusion
  1.2 0.1 broadcast_and_fusion
  1.3 1.1 %broadcast_select_fusion = bf16[2,2,256,256]{3,2,1,0:T(8,128)(2,1)S(1)} fusion(bf16[2,2,256,256]{3,2,1,0:T(8,128)(2,1)} %param.5, pred[2,256,256]{2,1,0:T(8,128)(4,1)S(1)} %broadcast_and_fusion), kind=kLoop, calls=%fused_computation.10 | loop fusion | flops 262144 | bytes 1179648 | tf_op jit(solution)/shard_map/jit(_where)/select_n | solution.py:29
  2.5 3.4 %collective-permute-start = (bf16[2,1,256,256]{3,2,1,0:T(8,128)(2,1)S(1)}, bf16[2,1,256,256]{3,2,1,0:T(8,128)(2,1)S(1)}, u32[]{:S(2)}, u32[]{:S(2)}) collective-permute-start(bf16[2,1,256,256]{3,2,1,0:T(8,128)(2,1)S(1)} %get-tuple-element.9), channel_id=1, source_target_pairs={{0,1},{1,2},{2,3},{3,4},{4,5},{5,6},{6,7},{7,8},{8,9},{9,10},{10,1... | collective-permute-start | bytes 786440 | tf_op jit(solution)/shard_map/ppermute | solution.py:14
  5.9 1.9 %collective-permute-start.1 = (bf16[2,1,256,256]{3,2,1,0:T(8,128)(2,1)S(1)}, bf16[2,1,256,256]{3,2,1,0:T(8,128)(2,1)S(1)}, u32[]{:S(2)}, u32[]{:S(2)}) collective-permute-start(bf16[2,1,256,256]{3,2,1,0:T(8,128)(2,1)S(1)} %get-tuple-element.10), channel_id=1, source_target_pairs={{1,0},{2,1},{3,2},{4,3},{5,4},{6,5},{7,6},{8,7},{9,8},{10,9},{11,1... | collective-permute-start | bytes 786440 | tf_op jit(solution)/shard_map/ppermute | solution.py:16
  7.8 0.0 copy-done.1
  7.8 1.3 %collective-permute-done = bf16[2,1,256,256]{3,2,1,0:T(8,128)(2,1)S(1)} collective-permute-done((bf16[2,1,256,256]{3,2,1,0:T(8,128)(2,1)S(1)}, bf16[2,1,256,256]{3,2,1,0:T(8,128)(2,1)S(1)}, u32[]{:S(2)}, u32[]{:S(2)}) %collective-permute-start) | collective-permute-done | bytes 262176 | tf_op jit(solution)/shard_map/ppermute | solution.py:14
  9.1 4.4 %collective-permute-done.1 = bf16[2,1,256,256]{3,2,1,0:T(8,128)(2,1)S(1)} collective-permute-done((bf16[2,1,256,256]{3,2,1,0:T(8,128)(2,1)S(1)}, bf16[2,1,256,256]{3,2,1,0:T(8,128)(2,1)S(1)}, u32[]{:S(2)}, u32[]{:S(2)}) %collective-permute-start.1) | collective-permute-done | bytes 262176 | tf_op jit(solution)/shard_map/ppermute | solution.py:16
  13.5 0.9 %pad_maximum_fusion.1 = (bf16[2,2,256,256]{3,2,1,0:T(8,128)(2,1)S(1)}, bf16[2,2,256,256]{3,2,1,0:T(8,128)(2,1)}) fusion(bf16[2,2,256,256]{3,2,1,0:T(8,128)(2,1)S(1)} %broadcast_select_fusion, bf16[2,1,256,256]{3,2,1,0:T(8,128)(2,1)S(1)} %collective-permute-done, bf16[2,1,256,256]{3,2,1,0:T(8,128)(2,1)S(1)} %collective-permute-done.1), kind=kLoop, calls=%fused_computation.9 | loop fusion | flops 524288 | bytes 2097152 | tf_op jit(solution)/shard_map/concatenate | solution.py:12
  14.4 0.0 copy-done
  14.4 5.5 %fusion = f32[2,2,256,256,1]{3,2,4,1,0:T(8,128)} fusion(pred[8]{0:T(512)(128)(4,1)S(1)} %get-tuple-element.12, pred[8]{0:T(512)(128)(4,1)S(1)} %get-tuple-element.11, bf16[2,2,256,256]{3,2,1,0:T(8,128)(2,1)} %get-tuple-element.8, bf16[2,2,256,256]{3,2,1,0:T(8,128)(2,1)S(1)} %broadcast_select_fusion, bf16[2,2,256,256]{3,2,1,0:T(8,128)(2,1)S(1)} %get-tuple-element.7, ...), kind=kOutput, calls=%fused_computation | convolution fusion | flops 2153775104 | bytes 6815760 | tf_op jit(solution)/shard_map/tvbij,tblj->vbil/dot_general | solution.py:41
  19.9 2.3 %copy.8 = f32[2,2,16,16,256]{4,3,0,1,2:T(8,128)} copy(f32[2,2,16,16,256]{4,3,2,0,1:T(8,128)} %bitcast.18) | data formatting | bytes 2097152 | tf_op jit(solution)/shard_map/reshape | solution.py:45
  22.3 11.2 %all-to-all-start = ((f32[2,2,16,16,256]{4,3,0,1,2:T(8,128)}), f32[2,2,16,16,256]{4,3,0,1,2:T(8,128)S(1)}, u32[]{:S(2)}, u32[]{:S(2)}) async-start(f32[2,2,16,16,256]{4,3,0,1,2:T(8,128)} %copy.8), calls=%async_computation | async-start | bytes 2097152 | tf_op jit(solution)/shard_map/all_to_all | solution.py:46
  33.5 28.1 %all-to-all-done = f32[2,2,16,16,256]{4,3,0,1,2:T(8,128)S(1)} async-done(((f32[2,2,16,16,256]{4,3,0,1,2:T(8,128)}), f32[2,2,16,16,256]{4,3,0,1,2:T(8,128)S(1)}, u32[]{:S(2)}, u32[]{:S(2)}) %all-to-all-start) | async-done | bytes 1048608 | tf_op jit(solution)/shard_map/all_to_all | solution.py:46
  61.6 0.1 reduce_sum.9
  61.7 0.6 %copy.10 = f32[2,2,16,256]{3,2,1,0:T(8,128)} copy(f32[2,2,16,256]{3,2,0,1:T(8,128)S(1)} %broadcast_select_fusion.1) | data formatting | bytes 131072 | tf_op jit(solution)/shard_map/jit(_where)/select_n | solution.py:50
  (4 shorter events, 0.1 us)
Async XLA Ops:
  0.0 14.4 %copy-start = (bf16[8,2,256,256]{3,2,1,0:T(8,128)(2,1)S(1)}, bf16[8,2,256,256]{3,2,1,0:T(8,128)(2,1)}, u32[]{:S(2)}) copy-start(bf16[8,2,256,256]{3,2,1,0:T(8,128)(2,1)} %param.7) | copy-start | bytes 6291460
  0.0 7.8 %copy-start.1 = (s32[8]{0:T(128)S(1)}, s32[8]{0:T(128)}, u32[]{:S(2)}) copy-start(s32[8]{0:T(128)} %param.9) | copy-start | bytes 100
  2.5 6.7 %collective-permute-start = (bf16[2,1,256,256]{3,2,1,0:T(8,128)(2,1)S(1)}, bf16[2,1,256,256]{3,2,1,0:T(8,128)(2,1)S(1)}, u32[]{:S(2)}, u32[]{:S(2)}) collective-permute-start(bf16[2,1,256,256]{3,2,1,0:T(8,128)(2,1)S(1)} %get-tuple-element.9), channel_id=1, source_target_pairs={{0,1},{1,2},{2,3},{3,4},{4,5},{5,6},{6,7},{7,8},{8,9},{9,10},{10,1... | collective-permute-start | bytes 786440 | tf_op jit(solution)/shard_map/ppermute | solution.py:14
  5.9 7.7 %collective-permute-start.1 = (bf16[2,1,256,256]{3,2,1,0:T(8,128)(2,1)S(1)}, bf16[2,1,256,256]{3,2,1,0:T(8,128)(2,1)S(1)}, u32[]{:S(2)}, u32[]{:S(2)}) collective-permute-start(bf16[2,1,256,256]{3,2,1,0:T(8,128)(2,1)S(1)} %get-tuple-element.10), channel_id=1, source_target_pairs={{1,0},{2,1},{3,2},{4,3},{5,4},{6,5},{7,6},{8,7},{9,8},{10,9},{11,1... | collective-permute-start | bytes 786440 | tf_op jit(solution)/shard_map/ppermute | solution.py:16
  22.3 39.4 %all-to-all-start = ((f32[2,2,16,16,256]{4,3,0,1,2:T(8,128)}), f32[2,2,16,16,256]{4,3,0,1,2:T(8,128)S(1)}, u32[]{:S(2)}, u32[]{:S(2)}) async-start(f32[2,2,16,16,256]{4,3,0,1,2:T(8,128)} %copy.8), calls=%async_computation | async-start | bytes 2097152 | tf_op jit(solution)/shard_map/all_to_all | solution.py:46

commit v2 on v1

--- a/solution.py
+++ b/solution.py
@@ -35,16 +35,18 @@
         padded[None, :, 0:block_count],
         jnp.where(shift == 0, padded[None, :, 1 : block_count + 1], padded[None, :, 2 : block_count + 2]),
     )
+    op_count = lax.axis_size("op")
+    share_rows = block_order // op_count
     half = jnp.einsum(
         "tbik,tvbkj->tvbij", left_ops, sources, preferred_element_type=jnp.float32
     ).astype(jnp.bfloat16)
     partial = jnp.einsum("tvbij,tblj->vbil", half, right_ops, preferred_element_type=jnp.float32)
 
-    op_count = lax.axis_size("op")
-    share_rows = block_order // op_count
-    shares = partial.reshape(partial.shape[0], block_count, op_count, share_rows, block_order)
+    shares = partial.astype(jnp.bfloat16).reshape(
+        partial.shape[0], block_count, op_count, share_rows, block_order
+    )
     received = lax.all_to_all(shares, "op", 2, 2, tiled=False)
-    own_share = received.sum(axis=2)
+    own_share = received.astype(jnp.float32).sum(axis=2)
     first_row = lax.axis_index("op") * share_rows
     live_share = lax.dynamic_slice_in_dim(live_mask, first_row, share_rows, 1)
     return jnp.where(live_share[None], own_share, jnp.zeros((), own_share.dtype))

time: 62.7 us -> 50.4 us (0.80)
  the two profiles are of different devices: /device:TPU:29 before, /device:TPU:87 now
where the time goes in v2:
time: 50.4 us; the launch traced here: 50.1 us
  waiting for transfers between devices  22.2 us (44%)
  starting transfers between devices  18.1 us (36%)
  matrix products  4.67 us (9%)
  local copies, waits for them, and re-layouts  2.61 us (5%)
  other arithmetic  2.48 us (5%)
    all_to_all x1, waiting for transfers between devices, per_device(): received = lax.all_to_all(shares, 'op', 2, 2, tiled=False)  10.3 us
    all_to_all x1, starting transfers between devices, per_device(): received = lax.all_to_all(shares, 'op', 2, 2, tiled=False)  10.2 us
    ppermute x1, waiting for transfers between devices, extended(): lax.ppermute(head, axis, [((i + 1) % count, i) for i in range(ends)])  7.85 us
    ppermute x1, starting transfers between devices, extended(): lax.ppermute(tail, axis, [(i, (i + 1) % count) for i in range(ends)])  5.9 us
    dot_general x1, matrix products, per_device(): jnp.einsum('tvbij,tblj->vbil', half, right_ops, preferred_element_type=jn...  4.67 us
    ppermute x1, waiting for transfers between devices, extended(): lax.ppermute(tail, axis, [(i, (i + 1) % count) for i in range(ends)])  4.1 us
    ppermute x1, starting transfers between devices, extended(): lax.ppermute(head, axis, [((i + 1) % count, i) for i in range(ends)])  1.92 us
    select_n x1, other arithmetic, per_device(): masked = jnp.where(live_mask[None], vectors, jnp.zeros((), vectors.dtype))  1.1 us
  transfers between devices with their start and end apart: 3, of which 3 were waited for; matrix products, arithmetic and copies ran while one was open for 0% of the time, Pallas kernels for 0%

profile of v2, /device:TPU:87, one launch (start us, length us, event | category | flops | bytes accessed | tf_op | source)
XLA Modules:
  0.0 50.1 jit_solution(4295197526792167296)
XLA Ops:
  0.0 0.0 copy-start
  0.0 0.0 copy-start.1
  0.0 1.1 %slice_reduce_fusion.1 = (s32[2]{0:T(128)S(1)}, s32[2]{0:T(128)S(1)}) fusion(s32[2,2]{1,0:T(2,128)} %param.8), kind=kLoop, calls=%fused_computation.19 | loop fusion | bytes 32 | tf_op jit(solution)/shard_map/slice | solution.py:26
  1.1 0.1 iota_compare_fusion
  1.2 0.1 broadcast_and_fusion
  1.3 1.1 %broadcast_select_fusion = bf16[2,2,256,256]{3,2,1,0:T(8,128)(2,1)S(1)} fusion(bf16[2,2,256,256]{3,2,1,0:T(8,128)(2,1)} %param.5, pred[2,256,256]{2,1,0:T(8,128)(4,1)S(1)} %broadcast_and_fusion), kind=kLoop, calls=%fused_computation.13 | loop fusion | flops 262144 | bytes 1179648 | tf_op jit(solution)/shard_map/jit(_where)/select_n | solution.py:29
  2.5 5.9 %collective-permute-start = (bf16[2,1,256,256]{3,2,1,0:T(8,128)(2,1)S(1)}, bf16[2,1,256,256]{3,2,1,0:T(8,128)(2,1)S(1)}, u32[]{:S(2)}, u32[]{:S(2)}) collective-permute-start(bf16[2,1,256,256]{3,2,1,0:T(8,128)(2,1)S(1)} %get-tuple-element.9), channel_id=1, source_target_pairs={{0,1},{1,2},{2,3},{3,4},{4,5},{5,6},{6,7},{7,8},{8,9},{9,10},{10,1... | collective-permute-start | bytes 786440 | tf_op jit(solution)/shard_map/ppermute | solution.py:14
  8.4 1.9 %collective-permute-start.1 = (bf16[2,1,256,256]{3,2,1,0:T(8,128)(2,1)S(1)}, bf16[2,1,256,256]{3,2,1,0:T(8,128)(2,1)S(1)}, u32[]{:S(2)}, u32[]{:S(2)}) collective-permute-start(bf16[2,1,256,256]{3,2,1,0:T(8,128)(2,1)S(1)} %get-tuple-element.10), channel_id=1, source_target_pairs={{1,0},{2,1},{3,2},{4,3},{5,4},{6,5},{7,6},{8,7},{9,8},{10,9},{11,1... | collective-permute-start | bytes 786440 | tf_op jit(solution)/shard_map/ppermute | solution.py:16
  10.3 0.0 copy-done.1
  10.3 4.1 %collective-permute-done = bf16[2,1,256,256]{3,2,1,0:T(8,128)(2,1)S(1)} collective-permute-done((bf16[2,1,256,256]{3,2,1,0:T(8,128)(2,1)S(1)}, bf16[2,1,256,256]{3,2,1,0:T(8,128)(2,1)S(1)}, u32[]{:S(2)}, u32[]{:S(2)}) %collective-permute-start) | collective-permute-done | bytes 262176 | tf_op jit(solution)/shard_map/ppermute | solution.py:14
  14.4 7.8 %collective-permute-done.1 = bf16[2,1,256,256]{3,2,1,0:T(8,128)(2,1)S(1)} collective-permute-done((bf16[2,1,256,256]{3,2,1,0:T(8,128)(2,1)S(1)}, bf16[2,1,256,256]{3,2,1,0:T(8,128)(2,1)S(1)}, u32[]{:S(2)}, u32[]{:S(2)}) %collective-permute-start.1) | collective-permute-done | bytes 262176 | tf_op jit(solution)/shard_map/ppermute | solution.py:16
  22.3 1.1 %pad_maximum_fusion.1 = (bf16[2,2,256,256]{3,2,1,0:T(8,128)(2,1)}, bf16[2,2,256,256]{3,2,1,0:T(8,128)(2,1)}) fusion(bf16[2,2,256,256]{3,2,1,0:T(8,128)(2,1)S(1)} %broadcast_select_fusion, bf16[2,1,256,256]{3,2,1,0:T(8,128)(2,1)S(1)} %collective-permute-done, bf16[2,1,256,256]{3,2,1,0:T(8,128)(2,1)S(1)} %collective-permute-done.1), kind=kLoop, calls=%fused_computation.12 | loop fusion | flops 524288 | bytes 2097152 | tf_op jit(solution)/shard_map/concatenate | solution.py:12
  23.3 0.0 copy-done
  23.3 4.7 %fusion.21 = bf16[2,2,256,256]{3,2,1,0:T(8,128)(2,1)S(1)} fusion(pred[8]{0:T(512)(128)(4,1)S(1)} %get-tuple-element.12, pred[8]{0:T(512)(128)(4,1)S(1)} %get-tuple-element.11, bf16[2,2,256,256]{3,2,1,0:T(8,128)(2,1)} %get-tuple-element.8, bf16[2,2,256,256]{3,2,1,0:T(8,128)(2,1)S(1)} %broadcast_select_fusion, bf16[2,2,256,256]{3,2,1,0:T(8,128)(2,1)} %get-tuple-element.7, ...), kind=kOutput, calls=%fused_computation.9 | convolution fusion | flops 2154037248 | bytes 6291472 | tf_op jit(solution)/shard_map/tvbij,tblj->vbil/dot_general | solution.py:43
  28.0 0.9 %copy.8 = bf16[2,2,16,16,256]{4,3,0,1,2:T(8,128)(2,1)} copy(bf16[2,2,16,16,256]{4,3,2,0,1:T(8,128)(2,1)S(1)} %bitcast.24) | data formatting | bytes 1048576 | tf_op jit(solution)/shard_map/reshape | solution.py:45
  28.9 10.2 %all-to-all-start = ((bf16[2,2,16,16,256]{4,3,0,1,2:T(8,128)(2,1)}), bf16[2,2,16,16,256]{4,3,0,1,2:T(8,128)(2,1)S(1)}, u32[]{:S(2)}, u32[]{:S(2)}) async-start(bf16[2,2,16,16,256]{4,3,0,1,2:T(8,128)(2,1)} %copy.8), calls=%async_computation | async-start | bytes 1048576 | tf_op jit(solution)/shard_map/all_to_all | solution.py:48
  39.1 10.3 %all-to-all-done = bf16[2,2,16,16,256]{4,3,0,1,2:T(8,128)(2,1)S(1)} async-done(((bf16[2,2,16,16,256]{4,3,0,1,2:T(8,128)(2,1)}), bf16[2,2,16,16,256]{4,3,0,1,2:T(8,128)(2,1)S(1)}, u32[]{:S(2)}, u32[]{:S(2)}) %all-to-all-start) | async-done | bytes 524320 | tf_op jit(solution)/shard_map/all_to_all | solution.py:48
  49.4 0.1 convert_reduce_fusion
  49.5 0.6 %copy.10 = f32[2,2,16,256]{3,2,1,0:T(8,128)} copy(f32[2,2,16,256]{3,2,0,1:T(8,128)S(1)} %broadcast_select_fusion.1) | data formatting | bytes 131072 | tf_op jit(solution)/shard_map/jit(_where)/select_n | solution.py:52
  (4 shorter events, 0.1 us)
Async XLA Ops:
  0.0 23.3 %copy-start = (bf16[8,2,256,256]{3,2,1,0:T(8,128)(2,1)S(1)}, bf16[8,2,256,256]{3,2,1,0:T(8,128)(2,1)}, u32[]{:S(2)}) copy-start(bf16[8,2,256,256]{3,2,1,0:T(8,128)(2,1)} %param.7) | copy-start | bytes 6291460
  0.0 10.3 %copy-start.1 = (s32[8]{0:T(128)S(1)}, s32[8]{0:T(128)}, u32[]{:S(2)}) copy-start(s32[8]{0:T(128)} %param.9) | copy-start | bytes 100
  2.5 12.0 %collective-permute-start = (bf16[2,1,256,256]{3,2,1,0:T(8,128)(2,1)S(1)}, bf16[2,1,256,256]{3,2,1,0:T(8,128)(2,1)S(1)}, u32[]{:S(2)}, u32[]{:S(2)}) collective-permute-start(bf16[2,1,256,256]{3,2,1,0:T(8,128)(2,1)S(1)} %get-tuple-element.9), channel_id=1, source_target_pairs={{0,1},{1,2},{2,3},{3,4},{4,5},{5,6},{6,7},{7,8},{8,9},{9,10},{10,1... | collective-permute-start | bytes 786440 | tf_op jit(solution)/shard_map/ppermute | solution.py:14
  8.4 13.9 %collective-permute-start.1 = (bf16[2,1,256,256]{3,2,1,0:T(8,128)(2,1)S(1)}, bf16[2,1,256,256]{3,2,1,0:T(8,128)(2,1)S(1)}, u32[]{:S(2)}, u32[]{:S(2)}) collective-permute-start(bf16[2,1,256,256]{3,2,1,0:T(8,128)(2,1)S(1)} %get-tuple-element.10), channel_id=1, source_target_pairs={{1,0},{2,1},{3,2},{4,3},{5,4},{6,5},{7,6},{8,7},{9,8},{10,9},{11,1... | collective-permute-start | bytes 786440 | tf_op jit(solution)/shard_map/ppermute | solution.py:16
  28.9 20.5 %all-to-all-start = ((bf16[2,2,16,16,256]{4,3,0,1,2:T(8,128)(2,1)}), bf16[2,2,16,16,256]{4,3,0,1,2:T(8,128)(2,1)S(1)}, u32[]{:S(2)}, u32[]{:S(2)}) async-start(bf16[2,2,16,16,256]{4,3,0,1,2:T(8,128)(2,1)} %copy.8), calls=%async_computation | async-start | bytes 1048576 | tf_op jit(solution)/shard_map/all_to_all | solution.py:48

commit v3 on v2

v3 whole, which is shorter than its diff:
```python
import jax
import jax.numpy as jnp
from jax import lax
from jax.sharding import PartitionSpec as P


def per_device(vectors, left_ops, right_ops, block_sizes, term_shifts):
    block_order = vectors.shape[2]
    row_index = jnp.arange(block_order, dtype=jnp.int32)
    live_mask = (row_index[None, :, None] < block_sizes[:, 0][:, None, None]) & (
        row_index[None, None, :] < block_sizes[:, 1][:, None, None]
    )
    masked = jnp.where(live_mask[None], vectors, jnp.zeros((), vectors.dtype))
    first, last = masked[:, 0], masked[:, 1]

    count = lax.axis_size("bond")
    below = lax.ppermute(last, "bond", [(i, i + 1) for i in range(count - 1)])
    above = lax.ppermute(first, "bond", [(i + 1, i) for i in range(count - 1)])

    shift = term_shifts[:, None, None, None]
    zero = jnp.zeros((), vectors.dtype)
    local_first = jnp.where(shift == 0, first[None], jnp.where(shift == -1, last[None], zero))
    local_last = jnp.where(shift == 1, first[None], jnp.where(shift == 0, last[None], zero))
    local_sources = jnp.stack([local_first, local_last], axis=2)
    half_local = jnp.einsum(
        "tbik,tvbkj->tvbij", left_ops, local_sources, preferred_element_type=jnp.float32
    )
    halo = jnp.stack([below, above], axis=1)
    half_halo = jnp.einsum("tbik,vbkj->tvbij", left_ops, halo, preferred_element_type=jnp.float32)
    from_halo = jnp.stack([term_shifts == 1, term_shifts == -1], axis=1)[:, None, :, None, None]
    half = jnp.where(from_halo, half_halo, half_local).astype(jnp.bfloat16)
    partial = jnp.einsum("tvbij,tblj->vbil", half, right_ops, preferred_element_type=jnp.float32)

    op_count = lax.axis_size("op")
    share_rows = block_order // op_count
    shares = partial.astype(jnp.bfloat16).reshape(
        partial.shape[0], partial.shape[1], op_count, share_rows, block_order
    )
    received = lax.all_to_all(shares, "op", 2, 2, tiled=False)
    own_share = received.astype(jnp.float32).sum(axis=2)
    first_row = lax.axis_index("op") * share_rows
    live_share = lax.dynamic_slice_in_dim(live_mask, first_row, share_rows, 1)
    return jnp.where(live_share[None], own_share, jnp.zeros((), own_share.dtype))


def solution(mesh):
    in_specs = (
        P(None, "bond", None, None),
        P("op", "bond", None, None),
        P("op", "bond", None, None),
        P("bond", None),
        P("op"),
    )
    out_specs = P(None, "bond", "op", None)
    return jax.shard_map(
        per_device, mesh=mesh, in_specs=in_specs, out_specs=out_specs, check_vma=False
    )
```

time: 50.4 us -> 51.1 us (1.014)
  the two profiles are of different devices: /device:TPU:87 before, /device:TPU:104 now
where the time goes in v3:
time: 51.1 us; the launch traced here: 50.8 us
  waiting for transfers between devices  20.7 us (41%)
  starting transfers between devices  17.6 us (34%)
  matrix products  7.95 us (16%)
  local copies, waits for them, and re-layouts  2.6 us (5%)
  other arithmetic  1.86 us (4%)
    all_to_all x1, waiting for transfers between devices, per_device(): received = lax.all_to_all(shares, 'op', 2, 2, tiled=False)  11.2 us
    all_to_all x1, starting transfers between devices, per_device(): received = lax.all_to_all(shares, 'op', 2, 2, tiled=False)  10.9 us
    ppermute x1, waiting for transfers between devices, per_device(): below = lax.ppermute(last, 'bond', [(i, i + 1) for i in range(count - 1)])  9.47 us
    dot_general x1, matrix products, per_device(): jnp.einsum('tvbij,tblj->vbil', half, right_ops, preferred_element_type=jn...  5.19 us
    ppermute x1, starting transfers between devices, per_device(): above = lax.ppermute(first, 'bond', [(i + 1, i) for i in range(count - 1)])  4.78 us
    dot_general x1, matrix products, per_device(): jnp.einsum('tbik,tvbkj->tvbij', left_ops, local_sources, preferred_elemen...  2.76 us
    ppermute x1, starting transfers between devices, per_device(): below = lax.ppermute(last, 'bond', [(i, i + 1) for i in range(count - 1)])  1.92 us
    select_n x1, other arithmetic, per_device(): masked = jnp.where(live_mask[None], vectors, jnp.zeros((), vectors.dtype))  1.1 us
  transfers between devices with their start and end apart: 3, of which 2 were waited for; matrix products, arithmetic and copies ran while one was open for 6% of the time, Pallas kernels for 0%

profile of v3, /device:TPU:104, one launch (start us, length us, event | category | flops | bytes accessed | tf_op | source)
XLA Modules:
  0.0 50.8 jit_solution(8206916270029402685)
XLA Ops:
  0.0 0.0 copy-start
  0.0 0.0 copy-start.1
  0.0 1.1 %slice_reduce_fusion.1 = (s32[2]{0:T(128)S(1)}, s32[2]{0:T(128)S(1)}) fusion(s32[2,2]{1,0:T(2,128)} %param.8), kind=kLoop, calls=%fused_computation.28 | loop fusion | bytes 32 | tf_op jit(solution)/shard_map/slice | solution.py:10
  1.1 0.1 iota_compare_fusion
  1.2 0.1 broadcast_and_fusion
  1.3 1.1 %broadcast_select_fusion = bf16[2,2,256,256]{3,2,1,0:T(8,128)(2,1)S(1)} fusion(bf16[2,2,256,256]{3,2,1,0:T(8,128)(2,1)} %param.5, pred[2,256,256]{2,1,0:T(8,128)(4,1)S(1)} %broadcast_and_fusion), kind=kLoop, calls=%fused_computation.19 | loop fusion | flops 262144 | bytes 1179648 | tf_op jit(solution)/shard_map/jit(_where)/select_n | solution.py:13
  2.5 4.8 %collective-permute-start.1 = (bf16[2,256,256]{2,1,0:T(8,128)(2,1)S(1)}, bf16[2,256,256]{2,1,0:T(8,128)(2,1)S(1)}, u32[]{:S(2)}, u32[]{:S(2)}) collective-permute-start(bf16[2,256,256]{2,1,0:T(8,128)(2,1)S(1)} %get-tuple-element.9), channel_id=1, source_target_pairs={{1,0},{2,1},{3,2},{4,3},{5,4},{6,5},{7,6},{8,7},{9,8},{10,9},{11,1... | collective-permute-start | bytes 786440 | tf_op jit(solution)/shard_map/ppermute | solution.py:18
  7.2 1.9 %collective-permute-start = (bf16[2,256,256]{2,1,0:T(8,128)(2,1)S(1)}, bf16[2,256,256]{2,1,0:T(8,128)(2,1)S(1)}, u32[]{:S(2)}, u32[]{:S(2)}) collective-permute-start(bf16[2,256,256]{2,1,0:T(8,128)(2,1)S(1)} %get-tuple-element.10), channel_id=1, source_target_pairs={{0,1},{1,2},{2,3},{3,4},{4,5},{5,6},{6,7},{7,8},{8,9},{9,10},{10,1... | collective-permute-start | bytes 786440 | tf_op jit(solution)/shard_map/ppermute | solution.py:17
  9.2 0.0 copy-done.1
  9.2 0.4 select_select_fusion.1
  9.6 0.0 copy-done
  9.6 2.8 %fusion.3 = bf16[8,2,2,256,256]{3,4,0,2,1:T(8,128)(2,1)} fusion(bf16[8,2,1,256,256]{4,3,2,1,0:T(8,128)(2,1)S(1)} %get-tuple-element.8, bf16[8,2,1,256,256]{4,3,2,1,0:T(8,128)(2,1)S(1)} %get-tuple-element.7, bf16[8,2,256,256]{3,2,1,0:T(8,128)(2,1)S(1)} %copy-done), kind=kOutput, calls=%fused_computation.4 | convolution fusion | flops 1075838976 | bytes 10485760 | tf_op jit(solution)/shard_map/tbik,tvbkj->tvbij/dot_general | solution.py:25
  12.4 0.0 collective-permute-done.1
  12.4 9.5 %collective-permute-done = bf16[2,256,256]{2,1,0:T(8,128)(2,1)S(1)} collective-permute-done((bf16[2,256,256]{2,1,0:T(8,128)(2,1)S(1)}, bf16[2,256,256]{2,1,0:T(8,128)(2,1)S(1)}, u32[]{:S(2)}, u32[]{:S(2)}) %collective-permute-start) | collective-permute-done | bytes 262176 | tf_op jit(solution)/shard_map/ppermute | solution.py:17
  21.9 5.2 %fusion.19 = bf16[2,2,256,256]{3,2,1,0:T(8,128)(2,1)S(1)} fusion(bf16[8,2,2,256,256]{3,4,0,2,1:T(8,128)(2,1)} %fusion.3, pred[8,2]{0,1:T(4,128)(4,1)S(1)} %pad_add_fusion, bf16[2,1,256,256]{3,2,0,1:T(8,128)(2,1)S(1)} %bitcast.55, bf16[2,1,256,256]{3,2,0,1:T(8,128)(2,1)S(1)} %bitcast.56, bf16[8,2,256,256]{3,2,1,0:T(8,128)(2,1)} %param.7, ...), kind=kOutput, calls=%fused_computation.14 | convolution fusion | flops 2150891520 | bytes 9437200 | tf_op jit(solution)/shard_map/tvbij,tblj->vbil/dot_general | solution.py:32
  27.1 0.9 %copy.10 = bf16[2,2,16,16,256]{4,3,0,1,2:T(8,128)(2,1)} copy(bf16[2,2,16,16,256]{4,3,2,0,1:T(8,128)(2,1)S(1)} %bitcast.54) | data formatting | bytes 1048576 | tf_op jit(solution)/shard_map/reshape | solution.py:36
  27.9 10.9 %all-to-all-start = ((bf16[2,2,16,16,256]{4,3,0,1,2:T(8,128)(2,1)}), bf16[2,2,16,16,256]{4,3,0,1,2:T(8,128)(2,1)S(1)}, u32[]{:S(2)}, u32[]{:S(2)}) async-start(bf16[2,2,16,16,256]{4,3,0,1,2:T(8,128)(2,1)} %copy.10), calls=%async_computation | async-start | bytes 1048576 | tf_op jit(solution)/shard_map/all_to_all | solution.py:39
  38.8 11.2 %all-to-all-done = bf16[2,2,16,16,256]{4,3,0,1,2:T(8,128)(2,1)S(1)} async-done(((bf16[2,2,16,16,256]{4,3,0,1,2:T(8,128)(2,1)}), bf16[2,2,16,16,256]{4,3,0,1,2:T(8,128)(2,1)S(1)}, u32[]{:S(2)}, u32[]{:S(2)}) %all-to-all-start) | async-done | bytes 524320 | tf_op jit(solution)/shard_map/all_to_all | solution.py:39
  50.1 0.1 convert_reduce_fusion
  50.2 0.6 %copy.12 = f32[2,2,16,256]{3,2,1,0:T(8,128)} copy(f32[2,2,16,256]{3,2,0,1:T(8,128)S(1)} %broadcast_select_fusion.1) | data formatting | bytes 131072 | tf_op jit(solution)/shard_map/jit(_where)/select_n | solution.py:43
  (5 shorter events, 0.1 us)
Async XLA Ops:
  0.0 9.6 %copy-start = (bf16[8,2,256,256]{3,2,1,0:T(8,128)(2,1)S(1)}, bf16[8,2,256,256]{3,2,1,0:T(8,128)(2,1)}, u32[]{:S(2)}) copy-start(bf16[8,2,256,256]{3,2,1,0:T(8,128)(2,1)} %param.6) | copy-start | bytes 6291460
  0.0 9.2 %copy-start.1 = (s32[8]{0:T(128)S(1)}, s32[8]{0:T(128)}, u32[]{:S(2)}) copy-start(s32[8]{0:T(128)} %param.9) | copy-start | bytes 100
  2.5 10.0 %collective-permute-start.1 = (bf16[2,256,256]{2,1,0:T(8,128)(2,1)S(1)}, bf16[2,256,256]{2,1,0:T(8,128)(2,1)S(1)}, u32[]{:S(2)}, u32[]{:S(2)}) collective-permute-start(bf16[2,256,256]{2,1,0:T(8,128)(2,1)S(1)} %get-tuple-element.9), channel_id=1, source_target_pairs={{1,0},{2,1},{3,2},{4,3},{5,4},{6,5},{7,6},{8,7},{9,8},{10,9},{11,1... | collective-permute-start | bytes 786440 | tf_op jit(solution)/shard_map/ppermute | solution.py:18
  7.2 14.6 %collective-permute-start = (bf16[2,256,256]{2,1,0:T(8,128)(2,1)S(1)}, bf16[2,256,256]{2,1,0:T(8,128)(2,1)S(1)}, u32[]{:S(2)}, u32[]{:S(2)}) collective-permute-start(bf16[2,256,256]{2,1,0:T(8,128)(2,1)S(1)} %get-tuple-element.10), channel_id=1, source_target_pairs={{0,1},{1,2},{2,3},{3,4},{4,5},{5,6},{6,7},{7,8},{8,9},{9,10},{10,1... | collective-permute-start | bytes 786440 | tf_op jit(solution)/shard_map/ppermute | solution.py:17
  27.9 22.1 %all-to-all-start = ((bf16[2,2,16,16,256]{4,3,0,1,2:T(8,128)(2,1)}), bf16[2,2,16,16,256]{4,3,0,1,2:T(8,128)(2,1)S(1)}, u32[]{:S(2)}, u32[]{:S(2)}) async-start(bf16[2,2,16,16,256]{4,3,0,1,2:T(8,128)(2,1)} %copy.10), calls=%async_computation | async-start | bytes 1048576 | tf_op jit(solution)/shard_map/all_to_all | solution.py:39

commit v4 on v3

--- a/solution.py
+++ b/solution.py
@@ -24,12 +24,22 @@
     local_sources = jnp.stack([local_first, local_last], axis=2)
     half_local = jnp.einsum(
         "tbik,tvbkj->tvbij", left_ops, local_sources, preferred_element_type=jnp.float32
+    ).astype(jnp.bfloat16)
+    partial_local = jnp.einsum(
+        "tvbij,tblj->vbil", half_local, right_ops, preferred_element_type=jnp.float32
     )
-    halo = jnp.stack([below, above], axis=1)
-    half_halo = jnp.einsum("tbik,vbkj->tvbij", left_ops, halo, preferred_element_type=jnp.float32)
-    from_halo = jnp.stack([term_shifts == 1, term_shifts == -1], axis=1)[:, None, :, None, None]
-    half = jnp.where(from_halo, half_halo, half_local).astype(jnp.bfloat16)
-    partial = jnp.einsum("tvbij,tblj->vbil", half, right_ops, preferred_element_type=jnp.float32)
+    partial_local = lax.optimization_barrier(partial_local)
+
+    def halo_part(block, halo, uses):
+        half = jnp.einsum(
+            "tik,vkj->tvij", left_ops[:, block], halo, preferred_element_type=jnp.float32
+        ).astype(jnp.bfloat16)
+        half = jnp.where(uses[:, None, None, None], half, jnp.zeros((), half.dtype))
+        return jnp.einsum("tvij,tlj->vil", half, right_ops[:, block], preferred_element_type=jnp.float32)
+
+    partial = partial_local + jnp.stack(
+        [halo_part(0, below, term_shifts == 1), halo_part(1, above, term_shifts == -1)], axis=1
+    )
 
     op_count = lax.axis_size("op")
     share_rows = block_order // op_count

time: 51.1 us -> 54.9 us (1.074)
  the two profiles are of different devices: /device:TPU:104 before, /device:TPU:31 now
where the time goes in v4:
time: 54.9 us; the launch traced here: 54.5 us
  starting transfers between devices  18.1 us (33%)
  waiting for transfers between devices  16.1 us (29%)
  matrix products  12.7 us (23%)
  other arithmetic  4.34 us (8%)
  local copies, waits for them, and re-layouts  3.22 us (6%)
    all_to_all x1, waiting for transfers between devices, per_device(): received = lax.all_to_all(shares, 'op', 2, 2, tiled=False)  15 us
    all_to_all x1, starting transfers between devices, per_device(): received = lax.all_to_all(shares, 'op', 2, 2, tiled=False)  11.2 us
    dot_general x2, matrix products, halo_part(): jnp.einsum('tvij,tlj->vil', half, right_ops[:, block], preferred_element_...  7.48 us
    dot_general x1, matrix products, per_device(): jnp.einsum('tvbij,tblj->vbil', half_local, right_ops, preferred_element_t...  5.2 us
    ppermute x1, starting transfers between devices, per_device(): below = lax.ppermute(last, 'bond', [(i, i + 1) for i in range(count - 1)])  4.99 us
    select_n x1, other arithmetic, per_device(): jnp.where(shift == 0, first[None], jnp.where(shift == -1, last[None], zero))  2.73 us
    ppermute x1, starting transfers between devices, per_device(): above = lax.ppermute(first, 'bond', [(i + 1, i) for i in range(count - 1)])  1.92 us
    select_n x1, other arithmetic, per_device(): masked = jnp.where(live_mask[None], vectors, jnp.zeros((), vectors.dtype))  1.1 us
  transfers between devices with their start and end apart: 3, of which 2 were waited for; matrix products, arithmetic and copies ran while one was open for 21% of the time, Pallas kernels for 0%

profile of v4, /device:TPU:31, one launch (start us, length us, event | category | flops | bytes accessed | tf_op | source)
XLA Modules:
  0.0 54.5 jit_solution(627005386836909550)
XLA Ops:
  0.0 0.0 copy-start
  0.0 1.0 %slice_reduce_fusion.1 = (s32[2]{0:T(128)S(1)}, s32[2]{0:T(128)S(1)}) fusion(s32[2,2]{1,0:T(2,128)} %param.8), kind=kLoop, calls=%fused_computation.48 | loop fusion | bytes 32 | tf_op jit(solution)/shard_map/slice | solution.py:10
  1.0 0.1 iota_compare_fusion
  1.0 0.1 broadcast_and_fusion
  1.2 1.1 %broadcast_select_fusion = bf16[2,2,256,256]{3,2,1,0:T(8,128)(2,1)S(1)} fusion(bf16[2,2,256,256]{3,2,1,0:T(8,128)(2,1)} %param.5, pred[2,256,256]{2,1,0:T(8,128)(4,1)S(1)} %broadcast_and_fusion), kind=kLoop, calls=%fused_computation.38 | loop fusion | flops 262144 | bytes 1179648 | tf_op jit(solution)/shard_map/jit(_where)/select_n | solution.py:13
  2.3 0.8 %slice_bitcast_fusion.1 = (bf16[2,256,256]{2,1,0:T(8,128)(2,1)S(1)}, bf16[2,256,256]{2,1,0:T(8,128)(2,1)}) fusion(bf16[2,2,256,256]{3,2,1,0:T(8,128)(2,1)S(1)} %broadcast_select_fusion), kind=kLoop, calls=%fused_computation.40 | loop fusion | bytes 1048576 | tf_op jit(solution)/shard_map/jit(_where)/broadcast_in_dim | solution.py:22
  3.1 5.0 %collective-permute-start = (bf16[2,256,256]{2,1,0:T(8,128)(2,1)}, bf16[2,256,256]{2,1,0:T(8,128)(2,1)}, u32[]{:S(2)}, u32[]{:S(2)}) collective-permute-start(bf16[2,256,256]{2,1,0:T(8,128)(2,1)} %get-tuple-element.10), channel_id=1, source_target_pairs={{0,1},{1,2},{2,3},{3,4},{4,5},{5,6},{6,7},{7,8},{8,9},{9,10},{10,1... | collective-permute-start | bytes 786440 | tf_op jit(solution)/shard_map/ppermute | solution.py:17
  8.1 1.9 %collective-permute-start.1 = (bf16[2,256,256]{2,1,0:T(8,128)(2,1)S(1)}, bf16[2,256,256]{2,1,0:T(8,128)(2,1)}, u32[]{:S(2)}, u32[]{:S(2)}) collective-permute-start(bf16[2,256,256]{2,1,0:T(8,128)(2,1)S(1)} %get-tuple-element.9), channel_id=1, source_target_pairs={{1,0},{2,1},{3,2},{4,3},{5,4},{6,5},{7,6},{8,7},{9,8},{10,9},{11,1... | collective-permute-start | bytes 786440 | tf_op jit(solution)/shard_map/ppermute | solution.py:18
  10.0 0.0 copy-done
  10.0 2.7 %select_select_fusion.1 = (bf16[8,2,1,256,256]{4,3,2,1,0:T(8,128)(2,1)S(1)}, bf16[8,2,1,256,256]{4,3,2,1,0:T(8,128)(2,1)}) fusion(pred[8]{0:T(512)(128)(4,1)S(1)} %get-tuple-element.11, pred[8]{0:T(512)(128)(4,1)S(1)} %get-tuple-element.12, bf16[2,256,256]{2,1,0:T(8,128)(2,1)} %get-tuple-element.10, bf16[2,256,256]{2,1,0:T(8,128)(2,1)S(1)} %get-tuple-element.9, ...), kind=kLoop, calls=%fused_computation.17 | loop fusion | flops 4194304 | bytes 4718616 | tf_op jit(solution)/shard_map/jit(_where)/select_n | solution.py:22
  12.8 5.2 %fusion.26 = f32[2,2,256,256]{3,2,0,1:T(8,128)S(1)} fusion(bf16[8,2,1,256,256]{4,3,2,1,0:T(8,128)(2,1)} %get-tuple-element.8, bf16[8,2,1,256,256]{4,3,2,1,0:T(8,128)(2,1)S(1)} %get-tuple-element.7, bf16[8,2,256,256]{3,2,1,0:T(8,128)(2,1)} %param.7, bf16[8,2,256,256]{3,2,1,0:T(8,128)(2,1)} %param.6), kind=kOutput, calls=%fused_computation.22 | convolution fusion | flops 2151677952 | bytes 9437184 | tf_op jit(solution)/shard_map/tvbij,tblj->vbil/dot_general | solution.py:28
  18.0 0.0 collective-permute-done
  18.0 3.7 %fusion.35 = f32[2,1,256,256]{3,2,0,1:T(8,128)S(1)} fusion(pred[8]{0:T(512)(128)(4,1)S(1)} %get-tuple-element.13, bf16[8,2,256,256]{3,2,1,0:T(8,128)(2,1)} %param.7, bf16[8,2,256,256]{3,2,1,0:T(8,128)(2,1)} %param.6, bf16[2,256,256]{2,1,0:T(8,128)(2,1)} %collective-permute-done), kind=kOutput, calls=%fused_computation.23 | convolution fusion | flops 1075838976 | bytes 2883592 | tf_op jit(solution)/shard_map/tvij,tlj->vil/dot_general | solution.py:38
  21.7 1.1 %collective-permute-done.1 = bf16[2,256,256]{2,1,0:T(8,128)(2,1)} collective-permute-done((bf16[2,256,256]{2,1,0:T(8,128)(2,1)S(1)}, bf16[2,256,256]{2,1,0:T(8,128)(2,1)}, u32[]{:S(2)}, u32[]{:S(2)}) %collective-permute-start.1) | collective-permute-done | bytes 262176 | tf_op jit(solution)/shard_map/ppermute | solution.py:18
  22.8 3.7 %fusion.38 = f32[2,1,256,256]{3,2,0,1:T(8,128)S(1)} fusion(pred[8]{0:T(512)(128)(4,1)S(1)} %get-tuple-element.11, bf16[8,2,256,256]{3,2,1,0:T(8,128)(2,1)} %param.7, bf16[8,2,256,256]{3,2,1,0:T(8,128)(2,1)} %param.6, bf16[2,256,256]{2,1,0:T(8,128)(2,1)} %collective-permute-done.1), kind=kOutput, calls=%fused_computation.24 | convolution fusion | flops 1075838976 | bytes 2883592 | tf_op jit(solution)/shard_map/tvij,tlj->vil/dot_general | solution.py:38
  26.5 0.2 fusion.41
  26.7 0.9 %copy.12 = bf16[2,2,16,16,256]{4,3,0,1,2:T(8,128)(2,1)} copy(bf16[2,2,16,16,256]{4,3,2,0,1:T(8,128)(2,1)S(1)} %bitcast.76) | data formatting | bytes 1048576 | tf_op jit(solution)/shard_map/reshape | solution.py:46
  27.6 11.2 %all-to-all-start = ((bf16[2,2,16,16,256]{4,3,0,1,2:T(8,128)(2,1)}), bf16[2,2,16,16,256]{4,3,0,1,2:T(8,128)(2,1)S(1)}, u32[]{:S(2)}, u32[]{:S(2)}) async-start(bf16[2,2,16,16,256]{4,3,0,1,2:T(8,128)(2,1)} %copy.12), calls=%async_computation | async-start | bytes 1048576 | tf_op jit(solution)/shard_map/all_to_all | solution.py:49
  38.8 15.0 %all-to-all-done = bf16[2,2,16,16,256]{4,3,0,1,2:T(8,128)(2,1)S(1)} async-done(((bf16[2,2,16,16,256]{4,3,0,1,2:T(8,128)(2,1)}), bf16[2,2,16,16,256]{4,3,0,1,2:T(8,128)(2,1)S(1)}, u32[]{:S(2)}, u32[]{:S(2)}) %all-to-all-start) | async-done | bytes 524320 | tf_op jit(solution)/shard_map/all_to_all | solution.py:49
  53.8 0.1 convert_reduce_fusion
  53.9 0.6 %copy.14 = f32[2,2,16,256]{3,2,1,0:T(8,128)} copy(f32[2,2,16,256]{3,2,0,1:T(8,128)S(1)} %broadcast_select_fusion.1) | data formatting | bytes 131072 | tf_op jit(solution)/shard_map/jit(_where)/select_n | solution.py:53
  (3 shorter events, 0.0 us)
Async XLA Ops:
  0.0 10.0 %copy-start = (s32[8]{0:T(128)S(1)}, s32[8]{0:T(128)}, u32[]{:S(2)}) copy-start(s32[8]{0:T(128)} %param.9) | copy-start | bytes 100
  3.1 14.9 %collective-permute-start = (bf16[2,256,256]{2,1,0:T(8,128)(2,1)}, bf16[2,256,256]{2,1,0:T(8,128)(2,1)}, u32[]{:S(2)}, u32[]{:S(2)}) collective-permute-start(bf16[2,256,256]{2,1,0:T(8,128)(2,1)} %get-tuple-element.10), channel_id=1, source_target_pairs={{0,1},{1,2},{2,3},{3,4},{4,5},{5,6},{6,7},{7,8},{8,9},{9,10},{10,1... | collective-permute-start | bytes 786440 | tf_op jit(solution)/shard_map/ppermute | solution.py:17
  8.1 14.7 %collective-permute-start.1 = (bf16[2,256,256]{2,1,0:T(8,128)(2,1)S(1)}, bf16[2,256,256]{2,1,0:T(8,128)(2,1)}, u32[]{:S(2)}, u32[]{:S(2)}) collective-permute-start(bf16[2,256,256]{2,1,0:T(8,128)(2,1)S(1)} %get-tuple-element.9), channel_id=1, source_target_pairs={{1,0},{2,1},{3,2},{4,3},{5,4},{6,5},{7,6},{8,7},{9,8},{10,9},{11,1... | collective-permute-start | bytes 786440 | tf_op jit(solution)/shard_map/ppermute | solution.py:18
  27.6 26.2 %all-to-all-start = ((bf16[2,2,16,16,256]{4,3,0,1,2:T(8,128)(2,1)}), bf16[2,2,16,16,256]{4,3,0,1,2:T(8,128)(2,1)S(1)}, u32[]{:S(2)}, u32[]{:S(2)}) async-start(bf16[2,2,16,16,256]{4,3,0,1,2:T(8,128)(2,1)} %copy.12), calls=%async_computation | async-start | bytes 1048576 | tf_op jit(solution)/shard_map/all_to_all | solution.py:49

commit v5 on v2

v5 whole, which is shorter than its diff:
```python
import jax
import jax.numpy as jnp
from jax import lax
from jax.sharding import PartitionSpec as P


def live_of(sizes, order):
    rows = jnp.arange(order, dtype=jnp.int32)
    return (rows[None, :, None] < sizes[:, 0][:, None, None]) & (rows[None, None, :] < sizes[:, 1][:, None, None])


def neighbours(vectors, block_sizes, order):
    count = lax.axis_size("bond")
    pad_rows = 16
    tag = jnp.zeros((vectors.shape[0], pad_rows, order), vectors.dtype)

    def packed(block):
        sizes = block_sizes[block].astype(vectors.dtype)
        return jnp.concatenate([vectors[:, block], tag.at[:, 0, 0:2].set(sizes)], axis=1)

    def unpacked(message):
        sizes = message[0, order, 0:2].astype(jnp.int32)
        live = live_of(sizes[None], order)[0]
        return jnp.where(live[None], message[:, :order], jnp.zeros((), vectors.dtype))

    below = lax.ppermute(packed(-1), "bond", [(i, i + 1) for i in range(count - 1)])
    above = lax.ppermute(packed(0), "bond", [(i + 1, i) for i in range(count - 1)])
    return unpacked(below), unpacked(above)


def per_device(vectors, left_ops, right_ops, block_sizes, term_shifts):
    block_count = vectors.shape[1]
    block_order = vectors.shape[2]
    below, above = neighbours(vectors, block_sizes, block_order)
    live_mask = live_of(block_sizes, block_order)
    masked = jnp.where(live_mask[None], vectors, jnp.zeros((), vectors.dtype))
    padded = jnp.concatenate([below[:, None], masked, above[:, None]], axis=1)

    shift = term_shifts[:, None, None, None, None]
    sources = jnp.where(
        shift == 1,
        padded[None, :, 0:block_count],
        jnp.where(shift == 0, padded[None, :, 1 : block_count + 1], padded[None, :, 2 : block_count + 2]),
    )
    half = jnp.einsum(
        "tbik,tvbkj->tvbij", left_ops, sources, preferred_element_type=jnp.float32
    ).astype(jnp.bfloat16)
    partial = jnp.einsum("tvbij,tblj->vbil", half, right_ops, preferred_element_type=jnp.float32)

    op_count = lax.axis_size("op")
    share_rows = block_order // op_count
    shares = partial.astype(jnp.bfloat16).reshape(
        partial.shape[0], block_count, op_count, share_rows, block_order
    )
    received = lax.all_to_all(shares, "op", 2, 2, tiled=False)
    own_share = received.astype(jnp.float32).sum(axis=2)
    first_row = lax.axis_index("op") * share_rows
    live_share = lax.dynamic_slice_in_dim(live_mask, first_row, share_rows, 1)
    return jnp.where(live_share[None], own_share, jnp.zeros((), own_share.dtype))


def solution(mesh):
    in_specs = (
        P(None, "bond", None, None),
        P("op", "bond", None, None),
        P("op", "bond", None, None),
        P("bond", None),
        P("op"),
    )
    out_specs = P(None, "bond", "op", None)
    return jax.shard_map(
        per_device, mesh=mesh, in_specs=in_specs, out_specs=out_specs, check_vma=False
    )
```

time: 50.4 us -> 55.1 us (1.093)
  the two profiles are of different devices: /device:TPU:87 before, /device:TPU:104 now
where the time goes in v5:
time: 55.1 us; the launch traced here: 54.8 us
  waiting for transfers between devices  23.1 us (42%)
  starting transfers between devices  17.6 us (32%)
  other arithmetic  5.12 us (9%)
  matrix products  4.67 us (8%)
  local copies, waits for them, and re-layouts  4.07 us (7%)
    all_to_all x1, waiting for transfers between devices, per_device(): received = lax.all_to_all(shares, 'op', 2, 2, tiled=False)  11.2 us
    all_to_all x1, starting transfers between devices, per_device(): received = lax.all_to_all(shares, 'op', 2, 2, tiled=False)  10.9 us
    ppermute x1, waiting for transfers between devices, neighbours(): lax.ppermute(packed(-1), 'bond', [(i, i + 1) for i in range(count - 1)])  10.1 us
    ppermute x1, starting transfers between devices, neighbours(): lax.ppermute(packed(0), 'bond', [(i + 1, i) for i in range(count - 1)])  4.78 us
    dot_general x1, matrix products, per_device(): jnp.einsum('tvbij,tblj->vbil', half, right_ops, preferred_element_type=jn...  4.67 us
    lt x3, other arithmetic, live_of(): rows[None, None, :] < sizes[:, 1][:, None, None]  2.61 us
    ppermute x1, starting transfers between devices, neighbours(): lax.ppermute(packed(-1), 'bond', [(i, i + 1) for i in range(count - 1)])  1.92 us
    ppermute x1, waiting for transfers between devices, neighbours(): lax.ppermute(packed(0), 'bond', [(i + 1, i) for i in range(count - 1)])  1.8 us
  transfers between devices with their start and end apart: 3, of which 3 were waited for; matrix products, arithmetic and copies ran while one was open for 2% of the time, Pallas kernels for 0%

profile of v5, /device:TPU:104, one launch (start us, length us, event | category | flops | bytes accessed | tf_op | source)
XLA Modules:
  0.0 54.8 jit_solution(9726018307609032639)
XLA Ops:
  0.0 0.0 copy-start
  0.0 0.0 copy-start.2
  0.0 0.0 copy-start.1
  0.0 0.0 copy-start.3
  0.0 0.8 %convert.6 = bf16[2,2]{1,0:T(2,128)(2,1)S(1)} convert(s32[2,2]{1,0:T(2,128)} %param.12) | non-fusion elementwise | flops 4 | bytes 24 | tf_op jit(solution)/shard_map/convert.3
  0.9 1.1 %slice_bitcast_fusion.1 = (bf16[2,256,256]{2,1,0:T(8,128)(2,1)S(1)}, bf16[2,256,256]{2,1,0:T(8,128)(2,1)S(1)}) fusion(bf16[2,2,256,256]{3,2,1,0:T(8,128)(2,1)} %param.9), kind=kLoop, calls=%fused_computation.21 | loop fusion | bytes 1048576 | tf_op jit(solution)/shard_map/squeeze | solution.py:19
  2.0 4.8 %collective-permute-start.1 = (bf16[2,272,256]{2,1,0:T(8,128)(2,1)S(1)}, bf16[2,272,256]{2,1,0:T(8,128)(2,1)S(1)}, u32[]{:S(2)}, u32[]{:S(2)}) collective-permute-start(bf16[2,272,256]{2,1,0:T(8,128)(2,1)S(1)} %pad_maximum_fusion.3), channel_id=1, source_target_pairs={{1,0},{2,1},{3,2},{4,3},{5,4},{6,5},{7,6},{8,7},{9,8},{10,9},{11,1... | collective-permute-start | bytes 835592 | tf_op jit(solution)/shard_map/ppermute | solution.py:27
  6.8 1.9 %collective-permute-start = (bf16[2,272,256]{2,1,0:T(8,128)(2,1)S(1)}, bf16[2,272,256]{2,1,0:T(8,128)(2,1)S(1)}, u32[]{:S(2)}, u32[]{:S(2)}) collective-permute-start(bf16[2,272,256]{2,1,0:T(8,128)(2,1)S(1)} %pad_maximum_fusion.2), channel_id=1, source_target_pairs={{0,1},{1,2},{2,3},{3,4},{4,5},{5,6},{6,7},{7,8},{8,9},{9,10},{10,1... | collective-permute-start | bytes 835592 | tf_op jit(solution)/shard_map/ppermute | solution.py:26
  8.8 0.0 copy-done.2
  8.8 0.2 slice_reduce_fusion.1
  8.9 0.1 iota_compare_fusion
  9.0 0.2 broadcast_and_fusion
  9.2 0.0 copy-done.3
  9.2 0.0 copy-done.1
  9.2 0.1 broadcast_select_fusion
  9.3 1.8 %collective-permute-done.1 = bf16[2,272,256]{2,1,0:T(8,128)(2,1)S(1)} collective-permute-done((bf16[2,272,256]{2,1,0:T(8,128)(2,1)S(1)}, bf16[2,272,256]{2,1,0:T(8,128)(2,1)S(1)}, u32[]{:S(2)}, u32[]{:S(2)}) %collective-permute-start.1) | collective-permute-done | bytes 278560 | tf_op jit(solution)/shard_map/ppermute | solution.py:27
  11.1 0.6 %fusion.36 = (s32[1,1]{1,0:T(1,128)}, s32[1,1]{1,0:T(1,128)}) fusion(s32[1,2]{1,0:T(1,128)S(1)} %fusion.32), kind=kLoop, calls=%fused_computation.43 | loop fusion | bytes 16 | tf_op jit(solution)/shard_map/slice | solution.py:9
  11.7 10.1 %collective-permute-done = bf16[2,272,256]{2,1,0:T(8,128)(2,1)S(1)} collective-permute-done((bf16[2,272,256]{2,1,0:T(8,128)(2,1)S(1)}, bf16[2,272,256]{2,1,0:T(8,128)(2,1)S(1)}, u32[]{:S(2)}, u32[]{:S(2)}) %collective-permute-start) | collective-permute-done | bytes 278560 | tf_op jit(solution)/shard_map/ppermute | solution.py:26
  21.8 0.6 %fusion.34 = (s32[1,1]{1,0:T(1,128)}, s32[1,1]{1,0:T(1,128)}) fusion(s32[1,2]{1,0:T(1,128)S(1)} %fusion.33), kind=kLoop, calls=%fused_computation.41 | loop fusion | bytes 16 | tf_op jit(solution)/shard_map/slice | solution.py:9
  22.5 1.3 %iota_compare_fusion.2 = (pred[256]{0:T(512)(128)(4,1)S(1)}, pred[256]{0:T(512)(128)(4,1)S(1)}) fusion(s32[]{:T(128)} %bitcast.11, s32[]{:T(128)} %bitcast.9), kind=kLoop, calls=%fused_computation.28 | loop fusion | flops 512 | bytes 520 | tf_op jit(solution)/shard_map/lt | solution.py:9
  23.7 0.1 broadcast_and_fusion.1
  23.8 1.3 %iota_compare_fusion.4 = (pred[256]{0:T(512)(128)(4,1)S(1)}, pred[256]{0:T(512)(128)(4,1)S(1)}) fusion(s32[]{:T(128)} %bitcast.4, s32[]{:T(128)} %bitcast.2), kind=kLoop, calls=%fused_computation.30 | loop fusion | flops 512 | bytes 520 | tf_op jit(solution)/shard_map/lt | solution.py:9
  25.1 0.1 broadcast_and_fusion.2
  25.3 1.1 %pad_maximum_fusion.1 = (bf16[2,2,256,256]{3,2,1,0:T(8,128)(2,1)}, bf16[2,2,256,256]{3,2,1,0:T(8,128)(2,1)}) fusion(bf16[2,2,256,256]{3,2,1,0:T(8,128)(2,1)S(1)} %broadcast_select_fusion, bf16[2,1,256,256]{3,2,1,0:T(8,128)(2,1)S(1)} %fusion.31, bf16[2,1,256,256]{3,2,1,0:T(8,128)(2,1)S(1)} %fusion.30), kind=kLoop, calls=%fused_computation.12 | loop fusion | flops 524288 | bytes 2097152 | tf_op jit(solution)/shard_map/concatenate | solution.py:37
  26.4 0.0 copy-done
  26.4 4.7 %fusion.21 = bf16[2,2,256,256]{3,2,1,0:T(8,128)(2,1)S(1)} fusion(pred[8]{0:T(512)(128)(4,1)S(1)} %get-tuple-element.42, pred[8]{0:T(512)(128)(4,1)S(1)} %get-tuple-element.41, bf16[2,2,256,256]{3,2,1,0:T(8,128)(2,1)} %get-tuple-element.32, bf16[2,2,256,256]{3,2,1,0:T(8,128)(2,1)S(1)} %broadcast_select_fusion, ...), kind=kOutput, calls=%fused_computation.9 | convolution fusion | flops 2154037248 | bytes 6291472 | tf_op jit(solution)/shard_map/tvbij,tblj->vbil/dot_general | solution.py:48
  31.1 0.9 %copy.14 = bf16[2,2,16,16,256]{4,3,0,1,2:T(8,128)(2,1)} copy(bf16[2,2,16,16,256]{4,3,2,0,1:T(8,128)(2,1)S(1)} %bitcast.52) | data formatting | bytes 1048576 | tf_op jit(solution)/shard_map/reshape | solution.py:52
  31.9 10.9 %all-to-all-start = ((bf16[2,2,16,16,256]{4,3,0,1,2:T(8,128)(2,1)}), bf16[2,2,16,16,256]{4,3,0,1,2:T(8,128)(2,1)S(1)}, u32[]{:S(2)}, u32[]{:S(2)}) async-start(bf16[2,2,16,16,256]{4,3,0,1,2:T(8,128)(2,1)} %copy.14), calls=%async_computation | async-start | bytes 1048576 | tf_op jit(solution)/shard_map/all_to_all | solution.py:55
  42.8 11.2 %all-to-all-done = bf16[2,2,16,16,256]{4,3,0,1,2:T(8,128)(2,1)S(1)} async-done(((bf16[2,2,16,16,256]{4,3,0,1,2:T(8,128)(2,1)}), bf16[2,2,16,16,256]{4,3,0,1,2:T(8,128)(2,1)S(1)}, u32[]{:S(2)}, u32[]{:S(2)}) %all-to-all-start) | async-done | bytes 524320 | tf_op jit(solution)/shard_map/all_to_all | solution.py:55
  54.0 0.1 convert_reduce_fusion
  54.1 0.6 %copy.16 = f32[2,2,16,256]{3,2,1,0:T(8,128)} copy(f32[2,2,16,256]{3,2,0,1:T(8,128)S(1)} %broadcast_select_fusion.1) | data formatting | bytes 131072 | tf_op jit(solution)/shard_map/jit(_where)/select_n | solution.py:59
  (14 shorter events, 0.2 us)
Async XLA Ops:
  0.0 26.4 %copy-start = (bf16[8,2,256,256]{3,2,1,0:T(8,128)(2,1)S(1)}, bf16[8,2,256,256]{3,2,1,0:T(8,128)(2,1)}, u32[]{:S(2)}) copy-start(bf16[8,2,256,256]{3,2,1,0:T(8,128)(2,1)} %param.11) | copy-start | bytes 6291460
  0.0 8.8 %copy-start.2 = (s32[2,2]{1,0:T(2,128)S(1)}, s32[2,2]{1,0:T(2,128)}, u32[]{:S(2)}) copy-start(s32[2,2]{1,0:T(2,128)} %param.12) | copy-start | bytes 52
  0.0 9.2 %copy-start.1 = (bf16[2,2,256,256]{3,2,1,0:T(8,128)(2,1)S(1)}, bf16[2,2,256,256]{3,2,1,0:T(8,128)(2,1)}, u32[]{:S(2)}) copy-start(bf16[2,2,256,256]{3,2,1,0:T(8,128)(2,1)} %param.9) | copy-start | bytes 1572868
  0.0 9.2 %copy-start.3 = (s32[8]{0:T(128)S(1)}, s32[8]{0:T(128)}, u32[]{:S(2)}) copy-start(s32[8]{0:T(128)} %param.13) | copy-start | bytes 100
  2.0 9.1 %collective-permute-start.1 = (bf16[2,272,256]{2,1,0:T(8,128)(2,1)S(1)}, bf16[2,272,256]{2,1,0:T(8,128)(2,1)S(1)}, u32[]{:S(2)}, u32[]{:S(2)}) collective-permute-start(bf16[2,272,256]{2,1,0:T(8,128)(2,1)S(1)} %pad_maximum_fusion.3), channel_id=1, source_target_pairs={{1,0},{2,1},{3,2},{4,3},{5,4},{6,5},{7,6},{8,7},{9,8},{10,9},{11,1... | collective-permute-start | bytes 835592 | tf_op jit(solution)/shard_map/ppermute | solution.py:27
  6.8 15.0 %collective-permute-start = (bf16[2,272,256]{2,1,0:T(8,128)(2,1)S(1)}, bf16[2,272,256]{2,1,0:T(8,128)(2,1)S(1)}, u32[]{:S(2)}, u32[]{:S(2)}) collective-permute-start(bf16[2,272,256]{2,1,0:T(8,128)(2,1)S(1)} %pad_maximum_fusion.2), channel_id=1, source_target_pairs={{0,1},{1,2},{2,3},{3,4},{4,5},{5,6},{6,7},{7,8},{8,9},{9,10},{10,1... | collective-permute-start | bytes 835592 | tf_op jit(solution)/shard_map/ppermute | solution.py:26
  31.9 22.1 %all-to-all-start = ((bf16[2,2,16,16,256]{4,3,0,1,2:T(8,128)(2,1)}), bf16[2,2,16,16,256]{4,3,0,1,2:T(8,128)(2,1)S(1)}, u32[]{:S(2)}, u32[]{:S(2)}) async-start(bf16[2,2,16,16,256]{4,3,0,1,2:T(8,128)(2,1)} %copy.14), calls=%async_computation | async-start | bytes 1048576 | tf_op jit(solution)/shard_map/all_to_all | solution.py:55

commit v6 on v1

--- a/solution.py
+++ b/solution.py
@@ -35,6 +35,8 @@
         padded[None, :, 0:block_count],
         jnp.where(shift == 0, padded[None, :, 1 : block_count + 1], padded[None, :, 2 : block_count + 2]),
     )
+    op_count = lax.axis_size("op")
+    share_rows = block_order // op_count
     half = jnp.einsum(
         "tbik,tvbkj->tvbij", left_ops, sources, preferred_element_type=jnp.float32
     ).astype(jnp.bfloat16)
@@ -43,8 +45,15 @@
     op_count = lax.axis_size("op")
     share_rows = block_order // op_count
     shares = partial.reshape(partial.shape[0], block_count, op_count, share_rows, block_order)
-    received = lax.all_to_all(shares, "op", 2, 2, tiled=False)
-    own_share = received.sum(axis=2)
+    shares = shares.transpose(2, 0, 1, 3, 4).reshape(op_count, -1)
+    largest = jnp.maximum(jnp.max(jnp.abs(shares), axis=1), jnp.float32(2.0**-100))
+    exponent = jnp.floor(jnp.log2(largest))
+    coded = (shares * jnp.exp2(14.0 - exponent)[:, None]).astype(jnp.float16)
+    lane = jnp.zeros((op_count, 128), jnp.float16).at[:, 0].set(exponent.astype(jnp.float16))
+    received = lax.all_to_all(jnp.concatenate([coded, lane], axis=1), "op", 0, 0, tiled=True)
+    scale = jnp.exp2(received[:, -128].astype(jnp.float32) - 14.0)
+    decoded = received[:, :-128].astype(jnp.float32) * scale[:, None]
+    own_share = decoded.sum(axis=0).reshape(partial.shape[0], block_count, share_rows, block_order)
     first_row = lax.axis_index("op") * share_rows
     live_share = lax.dynamic_slice_in_dim(live_mask, first_row, share_rows, 1)
     return jnp.where(live_share[None], own_share, jnp.zeros((), own_share.dtype))

time: 62.7 us -> 61.4 us (0.979)
  the two profiles are of different devices: /device:TPU:29 before, /device:TPU:87 now
where the time goes in v6:
time: 61.4 us; the launch traced here: 60.9 us
  waiting for transfers between devices  20.9 us (34%)
  starting transfers between devices  18.1 us (29%)
  local copies, waits for them, and re-layouts  10.3 us (17%)
  other arithmetic  7.12 us (12%)
  matrix products  4.48 us (7%)
    all_to_all x1, waiting for transfers between devices, per_device(): lax.all_to_all(jnp.concatenate([coded, lane], axis=1), 'op', 0, 0, tiled=...  10.4 us
    all_to_all x1, starting transfers between devices, per_device(): lax.all_to_all(jnp.concatenate([coded, lane], axis=1), 'op', 0, 0, tiled=...  10.2 us
    ppermute x1, waiting for transfers between devices, extended(): lax.ppermute(head, axis, [((i + 1) % count, i) for i in range(ends)])  7.95 us
    ppermute x1, starting transfers between devices, extended(): lax.ppermute(tail, axis, [(i, (i + 1) % count) for i in range(ends)])  5.9 us
    dot_general x1, matrix products, per_device(): jnp.einsum('tvbij,tblj->vbil', half, right_ops, preferred_element_type=jn...  4.48 us
    unnamed x9, local copies, waits for them, and re-layouts  4.47 us
    ppermute x1, waiting for transfers between devices, extended(): lax.ppermute(tail, axis, [(i, (i + 1) % count) for i in range(ends)])  2.48 us
    slice x1, local copies, waits for them, and re-layouts, per_device(): padded[None, :, 0:block_count]  2.06 us
  transfers between devices with their start and end apart: 3, of which 3 were waited for; matrix products, arithmetic and copies ran while one was open for 3% of the time, Pallas kernels for 0%

profile of v6, /device:TPU:87, one launch (start us, length us, event | category | flops | bytes accessed | tf_op | source)
XLA Modules:
  0.0 60.9 jit_solution(3516296907273992961)
XLA Ops:
  0.0 0.0 copy-start
  0.0 0.0 copy-start.1
  0.0 1.1 %slice_reduce_fusion.1 = (s32[2]{0:T(128)S(1)}, s32[2]{0:T(128)S(1)}) fusion(s32[2,2]{1,0:T(2,128)} %param.10), kind=kLoop, calls=%fused_computation.31 | loop fusion | bytes 32 | tf_op jit(solution)/shard_map/slice | solution.py:26
  1.1 0.1 iota_compare_fusion.1
  1.2 0.1 broadcast_and_fusion
  1.3 1.1 %broadcast_select_fusion = bf16[2,2,256,256]{3,2,1,0:T(8,128)(2,1)S(1)} fusion(bf16[2,2,256,256]{3,2,1,0:T(8,128)(2,1)} %param.7, pred[2,256,256]{2,1,0:T(8,128)(4,1)S(1)} %broadcast_and_fusion), kind=kLoop, calls=%fused_computation.23 | loop fusion | flops 262144 | bytes 1179648 | tf_op jit(solution)/shard_map/jit(_where)/select_n | solution.py:29
  2.5 5.9 %collective-permute-start = (bf16[2,1,256,256]{3,2,1,0:T(8,128)(2,1)S(1)}, bf16[2,1,256,256]{3,2,1,0:T(8,128)(2,1)S(1)}, u32[]{:S(2)}, u32[]{:S(2)}) collective-permute-start(bf16[2,1,256,256]{3,2,1,0:T(8,128)(2,1)S(1)} %get-tuple-element.21), channel_id=1, source_target_pairs={{0,1},{1,2},{2,3},{3,4},{4,5},{5,6},{6,7},{7,8},{8,9},{9,10},{10,1... | collective-permute-start | bytes 786440 | tf_op jit(solution)/shard_map/ppermute | solution.py:14
  8.4 1.9 %collective-permute-start.1 = (bf16[2,1,256,256]{3,2,1,0:T(8,128)(2,1)S(1)}, bf16[2,1,256,256]{3,2,1,0:T(8,128)(2,1)}, u32[]{:S(2)}, u32[]{:S(2)}) collective-permute-start(bf16[2,1,256,256]{3,2,1,0:T(8,128)(2,1)S(1)} %get-tuple-element.22), channel_id=1, source_target_pairs={{1,0},{2,1},{3,2},{4,3},{5,4},{6,5},{7,6},{8,7},{9,8},{10,9},{11,1... | collective-permute-start | bytes 786440 | tf_op jit(solution)/shard_map/ppermute | solution.py:16
  10.3 1.0 %copy.12 = bf16[2,2,256,256]{2,3,0,1:T(8,128)(2,1)} copy(bf16[2,2,256,256]{3,2,1,0:T(8,128)(2,1)S(1)} %broadcast_select_fusion) | data formatting | bytes 1048576 | tf_op jit(solution)/shard_map/jit(_where)/select_n | solution.py:29
  11.3 0.6 %compare_reduce_fusion = pred[]{:T(512)} fusion(), kind=kLoop, calls=%fused_computation.29 | loop fusion | flops 5 | bytes 1 | tf_op jit(solution)/shard_map/reduce.1
  11.9 0.0 copy-done.1
  11.9 2.5 %collective-permute-done = bf16[2,1,256,256]{3,2,1,0:T(8,128)(2,1)S(1)} collective-permute-done((bf16[2,1,256,256]{3,2,1,0:T(8,128)(2,1)S(1)}, bf16[2,1,256,256]{3,2,1,0:T(8,128)(2,1)S(1)}, u32[]{:S(2)}, u32[]{:S(2)}) %collective-permute-start) | collective-permute-done | bytes 262176 | tf_op jit(solution)/shard_map/ppermute | solution.py:14
  14.4 8.0 %collective-permute-done.1 = bf16[2,1,256,256]{3,2,1,0:T(8,128)(2,1)} collective-permute-done((bf16[2,1,256,256]{3,2,1,0:T(8,128)(2,1)S(1)}, bf16[2,1,256,256]{3,2,1,0:T(8,128)(2,1)}, u32[]{:S(2)}, u32[]{:S(2)}) %collective-permute-start.1) | collective-permute-done | bytes 262176 | tf_op jit(solution)/shard_map/ppermute | solution.py:16
  22.4 1.9 %pad_maximum_fusion.1 = (bf16[2,2,256,256]{3,2,1,0:T(8,128)(2,1)}, bf16[2,2,256,256]{3,2,1,0:T(8,128)(2,1)S(1)}) fusion(bf16[2,2,256,256]{3,2,1,0:T(8,128)(2,1)S(1)} %broadcast_select_fusion, bf16[2,1,256,256]{3,2,1,0:T(8,128)(2,1)S(1)} %collective-permute-done, bf16[2,1,256,256]{3,2,1,0:T(8,128)(2,1)} %collective-permute-done.1), kind=kLoop, calls=%fused_computation.22 | loop fusion | flops 524288 | bytes 2097152 | tf_op jit(solution)/shard_map/concatenate | solution.py:12
  24.2 2.1 %copy.11 = bf16[2,2,256,256]{2,3,0,1:T(8,128)(2,1)} copy(bf16[2,2,256,256]{3,2,1,0:T(8,128)(2,1)} %get-tuple-element.19) | data formatting | bytes 1048576 | tf_op jit(solution)/shard_map/slice | solution.py:35
  26.3 1.0 %copy.13 = bf16[2,2,256,256]{2,3,0,1:T(8,128)(2,1)} copy(bf16[2,2,256,256]{3,2,1,0:T(8,128)(2,1)S(1)} %get-tuple-element.20) | data formatting | bytes 1048576 | tf_op jit(solution)/shard_map/slice | solution.py:36
  27.3 0.0 copy-done
  27.3 4.5 %fusion = f32[2,2,256,256,1]{3,2,4,1,0:T(8,128)S(1)} fusion(pred[8]{0:T(512)(128)(4,1)S(1)} %get-tuple-element.24, pred[8]{0:T(512)(128)(4,1)S(1)} %get-tuple-element.23, bf16[2,2,256,256]{2,3,0,1:T(8,128)(2,1)} %copy.13, bf16[2,2,256,256]{2,3,0,1:T(8,128)(2,1)} %copy.12, bf16[2,2,256,256]{2,3,0,1:T(8,128)(2,1)} %copy.11, ...), kind=kOutput, calls=%fused_computation | convolution fusion | flops 2153775104 | bytes 6815760 | tf_op jit(solution)/shard_map/tvbij,tblj->vbil/dot_general | solution.py:43
  31.8 0.2 abs_reduce_fusion
  32.0 0.1 copy.17
  32.1 0.6 %copy.30 = f32[2,8,64,256]{3,1,2,0:T(8,128)S(1)} copy(f32[2,8,64,256]{3,2,1,0:T(8,128)S(1)} %bitcast.33) | data formatting | bytes 2097152
  32.7 0.7 %fusion.25 = f16[16,1]{0,1:T(2,128)(2,1)S(1)} fusion(pred[]{:T(512)} %compare_reduce_fusion, f32[16]{0:T(128)S(1)} %abs_reduce_fusion), kind=kLoop, calls=%fused_computation.33 | loop fusion | flops 80 | bytes 97 | tf_op jit(solution)/shard_map/select.7
  33.4 0.1 copy.29
  33.5 0.2 multiply_convert_fusion
  33.7 0.1 fusion.24
  33.8 0.5 broadcast.186
  34.3 1.1 %reduce.15 = f16[16,16512]{1,0:T(8,128)(2,1)S(1)} reduce(f16[16,1,16512]{2,0,1:T(8,128)(2,1)S(1)} %fusion.24, f16[]{:T(256)} %broadcast.186), dimensions={1}, to_apply=%copy.19.reduce_sub_computation | reduce | bytes 1056770 | tf_op jit(solution)/shard_map/all_to_all | solution.py:53
  35.4 1.2 %reshape.139 = f16[16,2,8256]{2,1,0:T(2,128)(2,1)} reshape(f16[16,16512]{1,0:T(8,128)(2,1)S(1)} %reduce.15) | data formatting | bytes 1056768
  36.6 10.2 %all-to-all-start = ((f16[16,2,8256]{2,1,0:T(2,128)(2,1)}), f16[16,2,8256]{2,1,0:T(2,128)(2,1)}, u32[]{:S(2)}, u32[]{:S(2)}) async-start(f16[16,2,8256]{2,1,0:T(2,128)(2,1)} %reshape.139), calls=%async_computation | async-start | bytes 1064960 | tf_op jit(solution)/shard_map/all_to_all | solution.py:53
  46.9 10.4 %all-to-all-done = f16[16,2,8256]{2,1,0:T(2,128)(2,1)} async-done(((f16[16,2,8256]{2,1,0:T(2,128)(2,1)}), f16[16,2,8256]{2,1,0:T(2,128)(2,1)}, u32[]{:S(2)}, u32[]{:S(2)}) %all-to-all-start) | async-done | bytes 528416 | tf_op jit(solution)/shard_map/all_to_all | solution.py:53
  57.3 2.4 %reshape.140 = f16[16,1,16512]{2,1,0:T(2,128)(2,1)S(1)} reshape(f16[16,2,8256]{2,1,0:T(2,128)(2,1)} %all-to-all-done) | data formatting | bytes 1056768
  59.7 0.1 copy.40
  59.8 0.1 exponential_reduce_fusion
  59.9 0.3 multiply_reduce_fusion
  60.3 0.6 %broadcast_select_fusion.1 = f32[2,2,16,256]{3,2,1,0:T(8,128)} fusion(f32[2,2,16,256]{3,2,1,0:T(8,128)S(1)} %reshape.129, pred[2,16,256]{2,1,0:T(8,128)(4,1)S(1)} %constant_dynamic-slice_fusion), kind=kLoop, calls=%fused_computation.25 | loop fusion | flops 16384 | bytes 139264 | tf_op jit(solution)/shard_map/jit(_where)/select_n | solution.py:59
  (5 shorter events, 0.1 us)
Async XLA Ops:
  0.0 27.3 %copy-start = (bf16[8,2,256,256]{3,2,1,0:T(8,128)(2,1)S(1)}, bf16[8,2,256,256]{3,2,1,0:T(8,128)(2,1)}, u32[]{:S(2)}) copy-start(bf16[8,2,256,256]{3,2,1,0:T(8,128)(2,1)} %param.9) | copy-start | bytes 6291460
  0.0 11.9 %copy-start.1 = (s32[8]{0:T(128)S(1)}, s32[8]{0:T(128)}, u32[]{:S(2)}) copy-start(s32[8]{0:T(128)} %param.11) | copy-start | bytes 100
  2.5 12.0 %collective-permute-start = (bf16[2,1,256,256]{3,2,1,0:T(8,128)(2,1)S(1)}, bf16[2,1,256,256]{3,2,1,0:T(8,128)(2,1)S(1)}, u32[]{:S(2)}, u32[]{:S(2)}) collective-permute-start(bf16[2,1,256,256]{3,2,1,0:T(8,128)(2,1)S(1)} %get-tuple-element.21), channel_id=1, source_target_pairs={{0,1},{1,2},{2,3},{3,4},{4,5},{5,6},{6,7},{7,8},{8,9},{9,10},{10,1... | collective-permute-start | bytes 786440 | tf_op jit(solution)/shard_map/ppermute | solution.py:14
  8.4 14.0 %collective-permute-start.1 = (bf16[2,1,256,256]{3,2,1,0:T(8,128)(2,1)S(1)}, bf16[2,1,256,256]{3,2,1,0:T(8,128)(2,1)}, u32[]{:S(2)}, u32[]{:S(2)}) collective-permute-start(bf16[2,1,256,256]{3,2,1,0:T(8,128)(2,1)S(1)} %get-tuple-element.22), channel_id=1, source_target_pairs={{1,0},{2,1},{3,2},{4,3},{5,4},{6,5},{7,6},{8,7},{9,8},{10,9},{11,1... | collective-permute-start | bytes 786440 | tf_op jit(solution)/shard_map/ppermute | solution.py:16
  36.6 20.7 %all-to-all-start = ((f16[16,2,8256]{2,1,0:T(2,128)(2,1)}), f16[16,2,8256]{2,1,0:T(2,128)(2,1)}, u32[]{:S(2)}, u32[]{:S(2)}) async-start(f16[16,2,8256]{2,1,0:T(2,128)(2,1)} %reshape.139), calls=%async_computation | async-start | bytes 1064960 | tf_op jit(solution)/shard_map/all_to_all | solution.py:53

commit v7 on v1

--- a/solution.py
+++ b/solution.py
@@ -35,6 +35,8 @@
         padded[None, :, 0:block_count],
         jnp.where(shift == 0, padded[None, :, 1 : block_count + 1], padded[None, :, 2 : block_count + 2]),
     )
+    op_count = lax.axis_size("op")
+    share_rows = block_order // op_count
     half = jnp.einsum(
         "tbik,tvbkj->tvbij", left_ops, sources, preferred_element_type=jnp.float32
     ).astype(jnp.bfloat16)
@@ -42,9 +44,16 @@
 
     op_count = lax.axis_size("op")
     share_rows = block_order // op_count
-    shares = partial.reshape(partial.shape[0], block_count, op_count, share_rows, block_order)
-    received = lax.all_to_all(shares, "op", 2, 2, tiled=False)
-    own_share = received.sum(axis=2)
+    slabs = partial.shape[0] * block_count
+    shares = partial.reshape(slabs, op_count, share_rows, block_order)
+    largest = jnp.maximum(jnp.max(jnp.abs(shares), axis=(0, 2, 3)), jnp.float32(2.0**-100))
+    exponent = jnp.floor(jnp.log2(largest))
+    coded = (shares * jnp.exp2(14.0 - exponent)[None, :, None, None]).astype(jnp.float16)
+    tags = jnp.broadcast_to(exponent.astype(jnp.float16)[None, :, None, None], (1,) + shares.shape[1:])
+    received = lax.all_to_all(jnp.concatenate([coded, tags], axis=0), "op", 1, 1, tiled=True)
+    scale = jnp.exp2(received[slabs, :, 0, 0].astype(jnp.float32) - 14.0)
+    decoded = received[:slabs].astype(jnp.float32) * scale[None, :, None, None]
+    own_share = decoded.sum(axis=1).reshape(partial.shape[0], block_count, share_rows, block_order)
     first_row = lax.axis_index("op") * share_rows
     live_share = lax.dynamic_slice_in_dim(live_mask, first_row, share_rows, 1)
     return jnp.where(live_share[None], own_share, jnp.zeros((), own_share.dtype))

time: 62.7 us -> 57.2 us (0.912)
  the two profiles are of different devices: /device:TPU:29 before, /device:TPU:40 now
where the time goes in v7:
time: 57.2 us; the launch traced here: 56.9 us
  starting transfers between devices  21.6 us (38%)
  waiting for transfers between devices  19.7 us (34%)
  local copies, waits for them, and re-layouts  6.52 us (11%)
  matrix products  4.56 us (8%)
  other arithmetic  4.45 us (8%)
    all_to_all x1, waiting for transfers between devices, per_device(): lax.all_to_all(jnp.concatenate([coded, tags], axis=0), 'op', 1, 1, tiled=...  14.2 us
    all_to_all x1, starting transfers between devices, per_device(): lax.all_to_all(jnp.concatenate([coded, tags], axis=0), 'op', 1, 1, tiled=...  11.8 us
    ppermute x1, starting transfers between devices, extended(): lax.ppermute(head, axis, [((i + 1) % count, i) for i in range(ends)])  7.86 us
    dot_general x1, matrix products, per_device(): jnp.einsum('tvbij,tblj->vbil', half, right_ops, preferred_element_type=jn...  4.56 us
    ppermute x1, waiting for transfers between devices, extended(): lax.ppermute(head, axis, [((i + 1) % count, i) for i in range(ends)])  2.87 us
    ppermute x1, waiting for transfers between devices, extended(): lax.ppermute(tail, axis, [(i, (i + 1) % count) for i in range(ends)])  2.63 us
    slice x1, local copies, waits for them, and re-layouts, per_device(): padded[None, :, 0:block_count]  2.06 us
    ppermute x1, starting transfers between devices, extended(): lax.ppermute(tail, axis, [(i, (i + 1) % count) for i in range(ends)])  1.92 us
  transfers between devices with their start and end apart: 3, of which 3 were waited for; matrix products, arithmetic and copies ran while one was open for 2% of the time, Pallas kernels for 0%

profile of v7, /device:TPU:40, one launch (start us, length us, event | category | flops | bytes accessed | tf_op | source)
XLA Modules:
  0.0 56.9 jit_solution(14600833759775961572)
XLA Ops:
  0.0 0.0 copy-start
  0.0 0.0 copy-start.1
  0.0 1.1 %slice_reduce_fusion.1 = (s32[2]{0:T(128)S(1)}, s32[2]{0:T(128)S(1)}) fusion(s32[2,2]{1,0:T(2,128)} %param.8), kind=kLoop, calls=%fused_computation.26 | loop fusion | bytes 32 | tf_op jit(solution)/shard_map/slice | solution.py:26
  1.1 0.1 iota_compare_fusion
  1.2 0.1 broadcast_and_fusion
  1.3 1.1 %broadcast_select_fusion = bf16[2,2,256,256]{3,2,1,0:T(8,128)(2,1)S(1)} fusion(bf16[2,2,256,256]{3,2,1,0:T(8,128)(2,1)} %param.5, pred[2,256,256]{2,1,0:T(8,128)(4,1)S(1)} %broadcast_and_fusion), kind=kLoop, calls=%fused_computation.20 | loop fusion | flops 262144 | bytes 1179648 | tf_op jit(solution)/shard_map/jit(_where)/select_n | solution.py:29
  2.5 1.9 %collective-permute-start = (bf16[2,1,256,256]{3,2,1,0:T(8,128)(2,1)S(1)}, bf16[2,1,256,256]{3,2,1,0:T(8,128)(2,1)S(1)}, u32[]{:S(2)}, u32[]{:S(2)}) collective-permute-start(bf16[2,1,256,256]{3,2,1,0:T(8,128)(2,1)S(1)} %get-tuple-element.9), channel_id=1, source_target_pairs={{0,1},{1,2},{2,3},{3,4},{4,5},{5,6},{6,7},{7,8},{8,9},{9,10},{10,1... | collective-permute-start | bytes 786440 | tf_op jit(solution)/shard_map/ppermute | solution.py:14
  4.4 7.9 %collective-permute-start.1 = (bf16[2,1,256,256]{3,2,1,0:T(8,128)(2,1)S(1)}, bf16[2,1,256,256]{3,2,1,0:T(8,128)(2,1)}, u32[]{:S(2)}, u32[]{:S(2)}) collective-permute-start(bf16[2,1,256,256]{3,2,1,0:T(8,128)(2,1)S(1)} %get-tuple-element.10), channel_id=1, source_target_pairs={{1,0},{2,1},{3,2},{4,3},{5,4},{6,5},{7,6},{8,7},{9,8},{10,9},{11,1... | collective-permute-start | bytes 786440 | tf_op jit(solution)/shard_map/ppermute | solution.py:16
  12.3 1.0 %copy.33 = bf16[2,2,256,256]{2,3,0,1:T(8,128)(2,1)} copy(bf16[2,2,256,256]{3,2,1,0:T(8,128)(2,1)S(1)} %broadcast_select_fusion) | data formatting | bytes 1048576 | tf_op jit(solution)/shard_map/jit(_where)/select_n | solution.py:29
  13.3 0.0 copy-done.1
  13.3 2.6 %collective-permute-done = bf16[2,1,256,256]{3,2,1,0:T(8,128)(2,1)S(1)} collective-permute-done((bf16[2,1,256,256]{3,2,1,0:T(8,128)(2,1)S(1)}, bf16[2,1,256,256]{3,2,1,0:T(8,128)(2,1)S(1)}, u32[]{:S(2)}, u32[]{:S(2)}) %collective-permute-start) | collective-permute-done | bytes 262176 | tf_op jit(solution)/shard_map/ppermute | solution.py:14
  15.9 2.9 %collective-permute-done.1 = bf16[2,1,256,256]{3,2,1,0:T(8,128)(2,1)} collective-permute-done((bf16[2,1,256,256]{3,2,1,0:T(8,128)(2,1)S(1)}, bf16[2,1,256,256]{3,2,1,0:T(8,128)(2,1)}, u32[]{:S(2)}, u32[]{:S(2)}) %collective-permute-start.1) | collective-permute-done | bytes 262176 | tf_op jit(solution)/shard_map/ppermute | solution.py:16
  18.8 1.9 %pad_maximum_fusion.2 = (bf16[2,2,256,256]{3,2,1,0:T(8,128)(2,1)}, bf16[2,2,256,256]{3,2,1,0:T(8,128)(2,1)S(1)}) fusion(bf16[2,2,256,256]{3,2,1,0:T(8,128)(2,1)S(1)} %broadcast_select_fusion, bf16[2,1,256,256]{3,2,1,0:T(8,128)(2,1)S(1)} %collective-permute-done, bf16[2,1,256,256]{3,2,1,0:T(8,128)(2,1)} %collective-permute-done.1), kind=kLoop, calls=%fused_computation.19 | loop fusion | flops 524288 | bytes 2097152 | tf_op jit(solution)/shard_map/concatenate | solution.py:12
  20.6 2.1 %copy.32 = bf16[2,2,256,256]{2,3,0,1:T(8,128)(2,1)} copy(bf16[2,2,256,256]{3,2,1,0:T(8,128)(2,1)} %get-tuple-element.7) | data formatting | bytes 1048576 | tf_op jit(solution)/shard_map/slice | solution.py:35
  22.7 1.0 %copy.34 = bf16[2,2,256,256]{2,3,0,1:T(8,128)(2,1)} copy(bf16[2,2,256,256]{3,2,1,0:T(8,128)(2,1)S(1)} %get-tuple-element.8) | data formatting | bytes 1048576 | tf_op jit(solution)/shard_map/slice | solution.py:36
  23.7 0.0 copy-done
  23.7 4.6 %abs_reduce_fusion = (f32[256]{0:T(256)S(1)}, f32[2,2,256,256]{3,2,0,1:T(8,128)S(1)}) fusion(pred[8]{0:T(512)(128)(4,1)S(1)} %get-tuple-element.14, pred[8]{0:T(512)(128)(4,1)S(1)} %get-tuple-element.13, bf16[2,2,256,256]{2,3,0,1:T(8,128)(2,1)} %copy.34, bf16[2,2,256,256]{2,3,0,1:T(8,128)(2,1)} %copy.33, bf16[2,2,256,256]{2,3,0,1:T(8,128)(2,1)} %copy.32, ...), kind=kOutput, calls=%fused_computation.16 | convolution fusion | flops 2154299136 | bytes 6816784 | tf_op jit(solution)/shard_map/tvbij,tblj->vbil/dot_general | solution.py:43
  28.3 0.1 reduce_max.14
  28.3 0.1 reduce_max.18
  28.5 0.1 copy.38
  28.6 0.2 multiply_convert_fusion
  28.7 0.1 broadcast_in_dim.88
  28.8 0.2 pad_maximum_fusion
  29.0 1.0 %copy.39 = f16[5,16,16,256]{3,2,0,1:T(8,128)(2,1)} copy(f16[5,16,16,256]{3,2,1,0:T(8,128)(2,1)S(1)} %pad_maximum_fusion) | data formatting | bytes 1310720 | tf_op jit(solution)/shard_map/concatenate | solution.py:53
  30.0 11.8 %all-to-all-start = ((f16[5,16,16,256]{3,2,0,1:T(8,128)(2,1)}), f16[5,16,16,256]{3,2,0,1:T(8,128)(2,1)S(1)}, u32[]{:S(2)}, u32[]{:S(2)}) async-start(f16[5,16,16,256]{3,2,0,1:T(8,128)(2,1)} %copy.39), calls=%async_computation | async-start | bytes 1310720 | tf_op jit(solution)/shard_map/all_to_all | solution.py:53
  41.8 14.2 %all-to-all-done = f16[5,16,16,256]{3,2,0,1:T(8,128)(2,1)S(1)} async-done(((f16[5,16,16,256]{3,2,0,1:T(8,128)(2,1)}), f16[5,16,16,256]{3,2,0,1:T(8,128)(2,1)S(1)}, u32[]{:S(2)}, u32[]{:S(2)}) %all-to-all-start) | async-done | bytes 655392 | tf_op jit(solution)/shard_map/all_to_all | solution.py:53
  56.0 0.1 copy.49
  56.1 0.2 multiply_reduce_fusion
  56.2 0.6 %broadcast_select_fusion.1 = f32[2,2,16,256]{3,2,1,0:T(8,128)} fusion(f32[2,2,16,256]{3,2,1,0:T(8,128)S(1)} %bitcast.26, pred[2,16,256]{2,1,0:T(8,128)(4,1)S(1)} %constant_dynamic-slice_fusion), kind=kLoop, calls=%fused_computation.22 | loop fusion | flops 16384 | bytes 139264 | tf_op jit(solution)/shard_map/jit(_where)/select_n | solution.py:59
  (6 shorter events, 0.1 us)
Async XLA Ops:
  0.0 23.7 %copy-start = (bf16[8,2,256,256]{3,2,1,0:T(8,128)(2,1)S(1)}, bf16[8,2,256,256]{3,2,1,0:T(8,128)(2,1)}, u32[]{:S(2)}) copy-start(bf16[8,2,256,256]{3,2,1,0:T(8,128)(2,1)} %param.7) | copy-start | bytes 6291460
  0.0 13.3 %copy-start.1 = (s32[8]{0:T(128)S(1)}, s32[8]{0:T(128)}, u32[]{:S(2)}) copy-start(s32[8]{0:T(128)} %param.9) | copy-start | bytes 100
  2.5 13.4 %collective-permute-start = (bf16[2,1,256,256]{3,2,1,0:T(8,128)(2,1)S(1)}, bf16[2,1,256,256]{3,2,1,0:T(8,128)(2,1)S(1)}, u32[]{:S(2)}, u32[]{:S(2)}) collective-permute-start(bf16[2,1,256,256]{3,2,1,0:T(8,128)(2,1)S(1)} %get-tuple-element.9), channel_id=1, source_target_pairs={{0,1},{1,2},{2,3},{3,4},{4,5},{5,6},{6,7},{7,8},{8,9},{9,10},{10,1... | collective-permute-start | bytes 786440 | tf_op jit(solution)/shard_map/ppermute | solution.py:14
  4.4 14.4 %collective-permute-start.1 = (bf16[2,1,256,256]{3,2,1,0:T(8,128)(2,1)S(1)}, bf16[2,1,256,256]{3,2,1,0:T(8,128)(2,1)}, u32[]{:S(2)}, u32[]{:S(2)}) collective-permute-start(bf16[2,1,256,256]{3,2,1,0:T(8,128)(2,1)S(1)} %get-tuple-element.10), channel_id=1, source_target_pairs={{1,0},{2,1},{3,2},{4,3},{5,4},{6,5},{7,6},{8,7},{9,8},{10,9},{11,1... | collective-permute-start | bytes 786440 | tf_op jit(solution)/shard_map/ppermute | solution.py:16
  30.0 26.0 %all-to-all-start = ((f16[5,16,16,256]{3,2,0,1:T(8,128)(2,1)}), f16[5,16,16,256]{3,2,0,1:T(8,128)(2,1)S(1)}, u32[]{:S(2)}, u32[]{:S(2)}) async-start(f16[5,16,16,256]{3,2,0,1:T(8,128)(2,1)} %copy.39), calls=%async_computation | async-start | bytes 1310720 | tf_op jit(solution)/shard_map/all_to_all | solution.py:53

commit v8 on v2

--- a/solution.py
+++ b/solution.py
@@ -42,11 +42,16 @@
     ).astype(jnp.bfloat16)
     partial = jnp.einsum("tvbij,tblj->vbil", half, right_ops, preferred_element_type=jnp.float32)
 
-    shares = partial.astype(jnp.bfloat16).reshape(
+    op_count = lax.axis_size("op")
+    share_rows = block_order // op_count
+    source_max = jnp.max(jnp.abs(padded.astype(jnp.float32)))
+    bound = 65536.0 * 1.01 * source_max * left_ops.shape[0] * 0.03125 * 0.375
+    exponent = jnp.ceil(jnp.log2(jnp.maximum(bound, jnp.float32(2.0**-100))))
+    shares = (partial * jnp.exp2(14.0 - exponent)).astype(jnp.float16).reshape(
         partial.shape[0], block_count, op_count, share_rows, block_order
     )
     received = lax.all_to_all(shares, "op", 2, 2, tiled=False)
-    own_share = received.astype(jnp.float32).sum(axis=2)
+    own_share = received.astype(jnp.float32).sum(axis=2) * jnp.exp2(exponent - 14.0)
     first_row = lax.axis_index("op") * share_rows
     live_share = lax.dynamic_slice_in_dim(live_mask, first_row, share_rows, 1)
     return jnp.where(live_share[None], own_share, jnp.zeros((), own_share.dtype))

time: 50.4 us -> 51.9 us (1.030)
  between operations: 0.08 us -> 0.86 us
  other arithmetic: 2.48 us -> 3.25 us
    reduce_max x0 -> x1, other arithmetic: none -> 0.74 us  [per_device(): source_max = jnp.max(jnp.abs(padded.astype(jnp.float32)))]
where the time goes in v8:
time: 51.9 us; the launch traced here: 51.7 us
  waiting for transfers between devices  22.2 us (43%)
  starting transfers between devices  18.1 us (35%)
  matrix products  4.67 us (9%)
  other arithmetic  3.25 us (6%)
  local copies, waits for them, and re-layouts  2.66 us (5%)
  between operations  0.86 us (2%)
    all_to_all x1, starting transfers between devices, per_device(): received = lax.all_to_all(shares, 'op', 2, 2, tiled=False)  10.2 us
    all_to_all x1, waiting for transfers between devices, per_device(): received = lax.all_to_all(shares, 'op', 2, 2, tiled=False)  10.2 us
    ppermute x1, waiting for transfers between devices, extended(): lax.ppermute(head, axis, [((i + 1) % count, i) for i in range(ends)])  7.85 us
    ppermute x1, starting transfers between devices, extended(): lax.ppermute(tail, axis, [(i, (i + 1) % count) for i in range(ends)])  5.9 us
    dot_general x1, matrix products, per_device(): jnp.einsum('tvbij,tblj->vbil', half, right_ops, preferred_element_type=jn...  4.67 us
    ppermute x1, waiting for transfers between devices, extended(): lax.ppermute(tail, axis, [(i, (i + 1) % count) for i in range(ends)])  4.1 us
    ppermute x1, starting transfers between devices, extended(): lax.ppermute(head, axis, [((i + 1) % count, i) for i in range(ends)])  1.92 us
    select_n x1, other arithmetic, per_device(): masked = jnp.where(live_mask[None], vectors, jnp.zeros((), vectors.dtype))  1.1 us
  transfers between devices with their start and end apart: 3, of which 3 were waited for; matrix products, arithmetic and copies ran while one was open for 0% of the time, Pallas kernels for 0%

profile of v8, /device:TPU:87, one launch (start us, length us, event | category | flops | bytes accessed | tf_op | source)
XLA Modules:
  0.0 51.7 jit_solution(12376902510985000053)
XLA Ops:
  0.0 0.0 copy-start
  0.0 0.0 copy-start.1
  0.0 1.1 %slice_reduce_fusion.1 = (s32[2]{0:T(128)S(1)}, s32[2]{0:T(128)S(1)}) fusion(s32[2,2]{1,0:T(2,128)} %param.8), kind=kLoop, calls=%fused_computation.21 | loop fusion | bytes 32 | tf_op jit(solution)/shard_map/slice | solution.py:26
  1.1 0.1 iota_compare_fusion
  1.2 0.1 broadcast_and_fusion
  1.3 1.1 %broadcast_select_fusion = bf16[2,2,256,256]{3,2,1,0:T(8,128)(2,1)S(1)} fusion(bf16[2,2,256,256]{3,2,1,0:T(8,128)(2,1)} %param.5, pred[2,256,256]{2,1,0:T(8,128)(4,1)S(1)} %broadcast_and_fusion), kind=kLoop, calls=%fused_computation.15 | loop fusion | flops 262144 | bytes 1179648 | tf_op jit(solution)/shard_map/jit(_where)/select_n | solution.py:29
  2.5 5.9 %collective-permute-start = (bf16[2,1,256,256]{3,2,1,0:T(8,128)(2,1)S(1)}, bf16[2,1,256,256]{3,2,1,0:T(8,128)(2,1)S(1)}, u32[]{:S(2)}, u32[]{:S(2)}) collective-permute-start(bf16[2,1,256,256]{3,2,1,0:T(8,128)(2,1)S(1)} %get-tuple-element.9), channel_id=1, source_target_pairs={{0,1},{1,2},{2,3},{3,4},{4,5},{5,6},{6,7},{7,8},{8,9},{9,10},{10,1... | collective-permute-start | bytes 786440 | tf_op jit(solution)/shard_map/ppermute | solution.py:14
  8.4 1.9 %collective-permute-start.1 = (bf16[2,1,256,256]{3,2,1,0:T(8,128)(2,1)S(1)}, bf16[2,1,256,256]{3,2,1,0:T(8,128)(2,1)S(1)}, u32[]{:S(2)}, u32[]{:S(2)}) collective-permute-start(bf16[2,1,256,256]{3,2,1,0:T(8,128)(2,1)S(1)} %get-tuple-element.10), channel_id=1, source_target_pairs={{1,0},{2,1},{3,2},{4,3},{5,4},{6,5},{7,6},{8,7},{9,8},{10,9},{11,1... | collective-permute-start | bytes 786440 | tf_op jit(solution)/shard_map/ppermute | solution.py:16
  10.3 0.0 copy-done.1
  10.3 4.1 %collective-permute-done = bf16[2,1,256,256]{3,2,1,0:T(8,128)(2,1)S(1)} collective-permute-done((bf16[2,1,256,256]{3,2,1,0:T(8,128)(2,1)S(1)}, bf16[2,1,256,256]{3,2,1,0:T(8,128)(2,1)S(1)}, u32[]{:S(2)}, u32[]{:S(2)}) %collective-permute-start) | collective-permute-done | bytes 262176 | tf_op jit(solution)/shard_map/ppermute | solution.py:14
  14.4 7.8 %collective-permute-done.1 = bf16[2,1,256,256]{3,2,1,0:T(8,128)(2,1)S(1)} collective-permute-done((bf16[2,1,256,256]{3,2,1,0:T(8,128)(2,1)S(1)}, bf16[2,1,256,256]{3,2,1,0:T(8,128)(2,1)S(1)}, u32[]{:S(2)}, u32[]{:S(2)}) %collective-permute-start.1) | collective-permute-done | bytes 262176 | tf_op jit(solution)/shard_map/ppermute | solution.py:16
  22.3 0.7 %abs_reduce_fusion = f32[]{:T(128)} fusion(bf16[2,1,256,256]{3,2,1,0:T(8,128)(2,1)S(1)} %collective-permute-done.1, bf16[2,2,256,256]{3,2,1,0:T(8,128)(2,1)S(1)} %broadcast_select_fusion, bf16[2,1,256,256]{3,2,1,0:T(8,128)(2,1)S(1)} %collective-permute-done), kind=kLoop, calls=%fused_computation.8 | loop fusion | flops 2621439 | bytes 1048580 | tf_op jit(solution)/shard_map/reduce_max | solution.py:47
  23.7 1.1 %pad_maximum_fusion.1 = (bf16[2,2,256,256]{3,2,1,0:T(8,128)(2,1)}, bf16[2,2,256,256]{3,2,1,0:T(8,128)(2,1)}) fusion(bf16[2,2,256,256]{3,2,1,0:T(8,128)(2,1)S(1)} %broadcast_select_fusion, bf16[2,1,256,256]{3,2,1,0:T(8,128)(2,1)S(1)} %collective-permute-done, bf16[2,1,256,256]{3,2,1,0:T(8,128)(2,1)S(1)} %collective-permute-done.1), kind=kLoop, calls=%fused_computation.14 | loop fusion | flops 524288 | bytes 2097152 | tf_op jit(solution)/shard_map/concatenate | solution.py:12
  24.8 0.0 copy-done
  24.8 4.7 %fusion.30 = f16[2,2,256,256]{3,2,1,0:T(8,128)(2,1)S(1)} fusion(f32[]{:T(128)S(6)} %exp2.13, pred[8]{0:T(512)(128)(4,1)S(1)} %get-tuple-element.12, pred[8]{0:T(512)(128)(4,1)S(1)} %get-tuple-element.11, bf16[2,2,256,256]{3,2,1,0:T(8,128)(2,1)} %get-tuple-element.8, bf16[2,2,256,256]{3,2,1,0:T(8,128)(2,1)S(1)} %broadcast_select_fusion, ...), kind=kOutput, calls=%fused_computation.11 | convolution fusion | flops 2154299392 | bytes 6291476 | tf_op jit(solution)/shard_map/tvbij,tblj->vbil/dot_general | solution.py:43
  29.5 0.9 %copy.8 = f16[2,2,16,16,256]{4,3,0,1,2:T(8,128)(2,1)} copy(f16[2,2,16,16,256]{4,3,2,0,1:T(8,128)(2,1)S(1)} %bitcast.28) | data formatting | bytes 1048576 | tf_op jit(solution)/shard_map/reshape | solution.py:50
  30.4 10.2 %all-to-all-start = ((f16[2,2,16,16,256]{4,3,0,1,2:T(8,128)(2,1)}), f16[2,2,16,16,256]{4,3,0,1,2:T(8,128)(2,1)S(1)}, u32[]{:S(2)}, u32[]{:S(2)}) async-start(f16[2,2,16,16,256]{4,3,0,1,2:T(8,128)(2,1)} %copy.8), calls=%async_computation | async-start | bytes 1048576 | tf_op jit(solution)/shard_map/all_to_all | solution.py:53
  40.7 10.2 %all-to-all-done = f16[2,2,16,16,256]{4,3,0,1,2:T(8,128)(2,1)S(1)} async-done(((f16[2,2,16,16,256]{4,3,0,1,2:T(8,128)(2,1)}), f16[2,2,16,16,256]{4,3,0,1,2:T(8,128)(2,1)S(1)}, u32[]{:S(2)}, u32[]{:S(2)}) %all-to-all-start) | async-done | bytes 524320 | tf_op jit(solution)/shard_map/all_to_all | solution.py:53
  50.9 0.1 convert_reduce_fusion
  51.0 0.6 %copy.10 = f32[2,2,16,256]{3,2,1,0:T(8,128)} copy(f32[2,2,16,256]{3,2,0,1:T(8,128)S(1)} %multiply_select_fusion) | data formatting | bytes 131072 | tf_op jit(solution)/shard_map/jit(_where)/select_n | solution.py:57
  (4 shorter events, 0.1 us)
Async XLA Ops:
  0.0 24.8 %copy-start = (bf16[8,2,256,256]{3,2,1,0:T(8,128)(2,1)S(1)}, bf16[8,2,256,256]{3,2,1,0:T(8,128)(2,1)}, u32[]{:S(2)}) copy-start(bf16[8,2,256,256]{3,2,1,0:T(8,128)(2,1)} %param.7) | copy-start | bytes 6291460
  0.0 10.3 %copy-start.1 = (s32[8]{0:T(128)S(1)}, s32[8]{0:T(128)}, u32[]{:S(2)}) copy-start(s32[8]{0:T(128)} %param.9) | copy-start | bytes 100
  2.5 12.0 %collective-permute-start = (bf16[2,1,256,256]{3,2,1,0:T(8,128)(2,1)S(1)}, bf16[2,1,256,256]{3,2,1,0:T(8,128)(2,1)S(1)}, u32[]{:S(2)}, u32[]{:S(2)}) collective-permute-start(bf16[2,1,256,256]{3,2,1,0:T(8,128)(2,1)S(1)} %get-tuple-element.9), channel_id=1, source_target_pairs={{0,1},{1,2},{2,3},{3,4},{4,5},{5,6},{6,7},{7,8},{8,9},{9,10},{10,1... | collective-permute-start | bytes 786440 | tf_op jit(solution)/shard_map/ppermute | solution.py:14
  8.4 13.9 %collective-permute-start.1 = (bf16[2,1,256,256]{3,2,1,0:T(8,128)(2,1)S(1)}, bf16[2,1,256,256]{3,2,1,0:T(8,128)(2,1)S(1)}, u32[]{:S(2)}, u32[]{:S(2)}) collective-permute-start(bf16[2,1,256,256]{3,2,1,0:T(8,128)(2,1)S(1)} %get-tuple-element.10), channel_id=1, source_target_pairs={{1,0},{2,1},{3,2},{4,3},{5,4},{6,5},{7,6},{8,7},{9,8},{10,9},{11,1... | collective-permute-start | bytes 786440 | tf_op jit(solution)/shard_map/ppermute | solution.py:16
  30.4 20.5 %all-to-all-start = ((f16[2,2,16,16,256]{4,3,0,1,2:T(8,128)(2,1)}), f16[2,2,16,16,256]{4,3,0,1,2:T(8,128)(2,1)S(1)}, u32[]{:S(2)}, u32[]{:S(2)}) async-start(f16[2,2,16,16,256]{4,3,0,1,2:T(8,128)(2,1)} %copy.8), calls=%async_computation | async-start | bytes 1048576 | tf_op jit(solution)/shard_map/all_to_all | solution.py:53

commit v9 on v8

--- a/solution.py
+++ b/solution.py
@@ -2,21 +2,6 @@
 import jax.numpy as jnp
 from jax import lax
 from jax.sharding import PartitionSpec as P
-
-
-def extended(cells, axis, dim):
-    count = lax.axis_size(axis)
-    ends = count - 1
-    head = lax.slice_in_dim(cells, 0, 1, axis=dim)
-    tail = lax.slice_in_dim(cells, cells.shape[dim] - 1, cells.shape[dim], axis=dim)
-    return jnp.concatenate(
-        [
-            lax.ppermute(tail, axis, [(i, (i + 1) % count) for i in range(ends)]),
-            cells,
-            lax.ppermute(head, axis, [((i + 1) % count, i) for i in range(ends)]),
-        ],
-        axis=dim,
-    )
 
 
 def per_device(vectors, left_ops, right_ops, block_sizes, term_shifts):
@@ -27,14 +12,15 @@
         row_index[None, None, :] < block_sizes[:, 1][:, None, None]
     )
     masked = jnp.where(live_mask[None], vectors, jnp.zeros((), vectors.dtype))
-    padded = extended(masked, "bond", 1)
+    count = lax.axis_size("bond")
+    first, last = masked[:, 0], masked[:, 1]
+    below = lax.ppermute(last, "bond", [(i, i + 1) for i in range(count - 1)])
+    above = lax.ppermute(first, "bond", [(i + 1, i) for i in range(count - 1)])
 
-    shift = term_shifts[:, None, None, None, None]
-    sources = jnp.where(
-        shift == 1,
-        padded[None, :, 0:block_count],
-        jnp.where(shift == 0, padded[None, :, 1 : block_count + 1], padded[None, :, 2 : block_count + 2]),
-    )
+    shift = term_shifts[:, None, None, None]
+    source_first = jnp.where(shift == 1, below[None], jnp.where(shift == 0, first[None], last[None]))
+    source_last = jnp.where(shift == 1, first[None], jnp.where(shift == 0, last[None], above[None]))
+    sources = jnp.stack([source_first, source_last], axis=2)
     op_count = lax.axis_size("op")
     share_rows = block_order // op_count
     half = jnp.einsum(
@@ -44,7 +30,10 @@
 
     op_count = lax.axis_size("op")
     share_rows = block_order // op_count
-    source_max = jnp.max(jnp.abs(padded.astype(jnp.float32)))
+    source_max = jnp.maximum(
+        jnp.max(jnp.abs(masked.astype(jnp.float32))),
+        jnp.maximum(jnp.max(jnp.abs(below.astype(jnp.float32))), jnp.max(jnp.abs(above.astype(jnp.float32)))),
+    )
     bound = 65536.0 * 1.01 * source_max * left_ops.shape[0] * 0.03125 * 0.375
     exponent = jnp.ceil(jnp.log2(jnp.maximum(bound, jnp.float32(2.0**-100))))
     shares = (partial * jnp.exp2(14.0 - exponent)).astype(jnp.float16).reshape(

time: 51.9 us -> 55.7 us (1.073)
  other arithmetic: 3.25 us -> 5.97 us
  between operations: 0.86 us -> 2.1 us
  waiting for transfers between devices: 22.2 us -> 21.4 us
    reduce_max x1 -> x3, other arithmetic: 0.74 us -> 3.13 us  [the longest x1 1.79 us: per_device(): jnp.max(jnp.abs(masked.astype(jnp.float32)))]
    select_n x1, other arithmetic: 1.1 us -> 2.51 us  [per_device(): jnp.where(shift == 1, below[None], jnp.where(shift == 0, first[None], las...]
    concatenate x1 -> x0, other arithmetic: 1.08 us -> none  [extended(): jnp.concatenate([lax.ppermute(tail, axis, [(i, (i + 1) % count) for i in...]
    ppermute x2, waiting for transfers between devices: 11.9 us -> 11.2 us  [the longest x1 7.13 us: per_device(): above = lax.ppermute(first, 'bond', [(i + 1, i) for i in range(count - 1)])]
  transfers between devices with their start and end apart: 3 -> 3, of which waited for: 3 -> 3; matrix products, arithmetic and copies ran while one was open for 0% -> 1% of each run, Pallas kernels for 0% -> 0%
where the time goes in v9:
time: 55.7 us; the launch traced here: 55.4 us
  waiting for transfers between devices  21.4 us (38%)
  starting transfers between devices  18.1 us (32%)
  other arithmetic  5.97 us (11%)
  matrix products  5.2 us (9%)
  local copies, waits for them, and re-layouts  2.65 us (5%)
  between operations  2.1 us (4%)
    all_to_all x1, starting transfers between devices, per_device(): received = lax.all_to_all(shares, 'op', 2, 2, tiled=False)  10.2 us
    all_to_all x1, waiting for transfers between devices, per_device(): received = lax.all_to_all(shares, 'op', 2, 2, tiled=False)  10.2 us
    ppermute x1, waiting for transfers between devices, per_device(): above = lax.ppermute(first, 'bond', [(i + 1, i) for i in range(count - 1)])  7.13 us
    ppermute x1, starting transfers between devices, per_device(): below = lax.ppermute(last, 'bond', [(i, i + 1) for i in range(count - 1)])  5.9 us
    dot_general x1, matrix products, per_device(): jnp.einsum('tvbij,tblj->vbil', half, right_ops, preferred_element_type=jn...  5.2 us
    ppermute x1, waiting for transfers between devices, per_device(): below = lax.ppermute(last, 'bond', [(i, i + 1) for i in range(count - 1)])  4.1 us
    select_n x1, other arithmetic, per_device(): jnp.where(shift == 1, below[None], jnp.where(shift == 0, first[None], las...  2.51 us
    ppermute x1, starting transfers between devices, per_device(): above = lax.ppermute(first, 'bond', [(i + 1, i) for i in range(count - 1)])  1.92 us
  transfers between devices with their start and end apart: 3, of which 3 were waited for; matrix products, arithmetic and copies ran while one was open for 1% of the time, Pallas kernels for 0%

profile of v9, /device:TPU:87, one launch (start us, length us, event | category | flops | bytes accessed | tf_op | source)
XLA Modules:
  0.0 55.4 jit_solution(86727793226652730)
XLA Ops:
  0.0 0.0 copy-start
  0.0 0.0 copy-start.1
  0.0 1.1 %slice_reduce_fusion.1 = (s32[2]{0:T(128)S(1)}, s32[2]{0:T(128)S(1)}) fusion(s32[2,2]{1,0:T(2,128)} %param.8), kind=kLoop, calls=%fused_computation.25 | loop fusion | bytes 32 | tf_op jit(solution)/shard_map/slice | solution.py:11
  1.1 0.1 iota_compare_fusion
  1.2 0.1 broadcast_and_fusion
  1.3 1.8 %abs_reduce_fusion = (f32[]{:T(128)}, bf16[2,2,256,256]{3,2,1,0:T(8,128)(2,1)S(1)}) fusion(bf16[2,2,256,256]{3,2,1,0:T(8,128)(2,1)} %param.5, pred[2,256,256]{2,1,0:T(8,128)(4,1)S(1)} %broadcast_and_fusion), kind=kLoop, calls=%fused_computation.14 | loop fusion | flops 1048575 | bytes 1179652 | tf_op jit(solution)/shard_map/reduce_max | solution.py:34
  3.1 5.9 %collective-permute-start = (bf16[2,256,256]{2,1,0:T(8,128)(2,1)S(1)}, bf16[2,256,256]{2,1,0:T(8,128)(2,1)S(1)}, u32[]{:S(2)}, u32[]{:S(2)}) collective-permute-start(bf16[2,256,256]{2,1,0:T(8,128)(2,1)S(1)} %get-tuple-element.11), channel_id=1, source_target_pairs={{0,1},{1,2},{2,3},{3,4},{4,5},{5,6},{6,7},{7,8},{8,9},{9,10},{10,1... | collective-permute-start | bytes 786440 | tf_op jit(solution)/shard_map/ppermute | solution.py:17
  9.1 1.9 %collective-permute-start.1 = (bf16[2,256,256]{2,1,0:T(8,128)(2,1)S(1)}, bf16[2,256,256]{2,1,0:T(8,128)(2,1)S(1)}, u32[]{:S(2)}, u32[]{:S(2)}) collective-permute-start(bf16[2,256,256]{2,1,0:T(8,128)(2,1)S(1)} %get-tuple-element.12), channel_id=1, source_target_pairs={{1,0},{2,1},{3,2},{4,3},{5,4},{6,5},{7,6},{8,7},{9,8},{10,9},{11,1... | collective-permute-start | bytes 786440 | tf_op jit(solution)/shard_map/ppermute | solution.py:18
  11.0 0.0 copy-done.1
  11.0 4.1 %collective-permute-done = bf16[2,256,256]{2,1,0:T(8,128)(2,1)S(1)} collective-permute-done((bf16[2,256,256]{2,1,0:T(8,128)(2,1)S(1)}, bf16[2,256,256]{2,1,0:T(8,128)(2,1)S(1)}, u32[]{:S(2)}, u32[]{:S(2)}) %collective-permute-start) | collective-permute-done | bytes 262176 | tf_op jit(solution)/shard_map/ppermute | solution.py:17
  15.1 0.7 %abs_reduce_fusion.2 = f32[]{:T(128)} fusion(bf16[2,256,256]{2,1,0:T(8,128)(2,1)S(1)} %collective-permute-done), kind=kLoop, calls=%fused_computation.16 | loop fusion | flops 393215 | bytes 262148 | tf_op jit(solution)/shard_map/reduce_max | solution.py:35
  15.8 7.1 %collective-permute-done.1 = bf16[2,256,256]{2,1,0:T(8,128)(2,1)S(1)} collective-permute-done((bf16[2,256,256]{2,1,0:T(8,128)(2,1)S(1)}, bf16[2,256,256]{2,1,0:T(8,128)(2,1)S(1)}, u32[]{:S(2)}, u32[]{:S(2)}) %collective-permute-start.1) | collective-permute-done | bytes 262176 | tf_op jit(solution)/shard_map/ppermute | solution.py:18
  23.0 0.6 %abs_reduce_fusion.1 = f32[]{:T(128)} fusion(bf16[2,256,256]{2,1,0:T(8,128)(2,1)S(1)} %collective-permute-done.1), kind=kLoop, calls=%fused_computation.15 | loop fusion | flops 393215 | bytes 262148 | tf_op jit(solution)/shard_map/reduce_max | solution.py:35
  25.6 2.5 %select_select_fusion.1 = (bf16[8,2,1,256,256]{4,3,2,1,0:T(8,128)(2,1)}, bf16[8,2,1,256,256]{4,3,2,1,0:T(8,128)(2,1)}) fusion(pred[8]{0:T(512)(128)(4,1)S(1)} %get-tuple-element.14, pred[8]{0:T(512)(128)(4,1)S(1)} %get-tuple-element.13, bf16[2,256,256]{2,1,0:T(8,128)(2,1)S(1)} %get-tuple-element.11, bf16[2,256,256]{2,1,0:T(8,128)(2,1)S(1)} %get-tuple-element.12, ...), kind=kLoop, calls=%fused_computation.9 | loop fusion | flops 4194304 | bytes 5242896 | tf_op jit(solution)/shard_map/jit(_where)/select_n | solution.py:21
  28.1 0.0 copy-done
  28.1 5.2 %fusion.30 = f16[2,2,256,256]{3,2,1,0:T(8,128)(2,1)S(1)} fusion(f32[]{:T(128)S(6)} %exp2.13, bf16[8,2,1,256,256]{4,3,2,1,0:T(8,128)(2,1)} %get-tuple-element.10, bf16[8,2,1,256,256]{4,3,2,1,0:T(8,128)(2,1)} %get-tuple-element.9, bf16[8,2,256,256]{3,2,1,0:T(8,128)(2,1)S(1)} %copy-done, bf16[8,2,256,256]{3,2,1,0:T(8,128)(2,1)} %param.6), kind=kOutput, calls=%fused_computation.12 | convolution fusion | flops 2152202240 | bytes 8912900 | tf_op jit(solution)/shard_map/tvbij,tblj->vbil/dot_general | solution.py:29
  33.3 0.9 %copy.8 = f16[2,2,16,16,256]{4,3,0,1,2:T(8,128)(2,1)} copy(f16[2,2,16,16,256]{4,3,2,0,1:T(8,128)(2,1)S(1)} %bitcast.32) | data formatting | bytes 1048576 | tf_op jit(solution)/shard_map/reshape | solution.py:39
  34.2 10.2 %all-to-all-start = ((f16[2,2,16,16,256]{4,3,0,1,2:T(8,128)(2,1)}), f16[2,2,16,16,256]{4,3,0,1,2:T(8,128)(2,1)S(1)}, u32[]{:S(2)}, u32[]{:S(2)}) async-start(f16[2,2,16,16,256]{4,3,0,1,2:T(8,128)(2,1)} %copy.8), calls=%async_computation | async-start | bytes 1048576 | tf_op jit(solution)/shard_map/all_to_all | solution.py:42
  44.5 10.2 %all-to-all-done = f16[2,2,16,16,256]{4,3,0,1,2:T(8,128)(2,1)S(1)} async-done(((f16[2,2,16,16,256]{4,3,0,1,2:T(8,128)(2,1)}), f16[2,2,16,16,256]{4,3,0,1,2:T(8,128)(2,1)S(1)}, u32[]{:S(2)}, u32[]{:S(2)}) %all-to-all-start) | async-done | bytes 524320 | tf_op jit(solution)/shard_map/all_to_all | solution.py:42
  54.7 0.1 convert_reduce_fusion
  54.8 0.6 %copy.10 = f32[2,2,16,256]{3,2,1,0:T(8,128)} copy(f32[2,2,16,256]{3,2,0,1:T(8,128)S(1)} %multiply_select_fusion) | data formatting | bytes 131072 | tf_op jit(solution)/shard_map/jit(_where)/select_n | solution.py:46
  (4 shorter events, 0.1 us)
Async XLA Ops:
  0.0 28.1 %copy-start = (bf16[8,2,256,256]{3,2,1,0:T(8,128)(2,1)S(1)}, bf16[8,2,256,256]{3,2,1,0:T(8,128)(2,1)}, u32[]{:S(2)}) copy-start(bf16[8,2,256,256]{3,2,1,0:T(8,128)(2,1)} %param.7) | copy-start | bytes 6291460
  0.0 11.0 %copy-start.1 = (s32[8]{0:T(128)S(1)}, s32[8]{0:T(128)}, u32[]{:S(2)}) copy-start(s32[8]{0:T(128)} %param.9) | copy-start | bytes 100
  3.1 12.0 %collective-permute-start = (bf16[2,256,256]{2,1,0:T(8,128)(2,1)S(1)}, bf16[2,256,256]{2,1,0:T(8,128)(2,1)S(1)}, u32[]{:S(2)}, u32[]{:S(2)}) collective-permute-start(bf16[2,256,256]{2,1,0:T(8,128)(2,1)S(1)} %get-tuple-element.11), channel_id=1, source_target_pairs={{0,1},{1,2},{2,3},{3,4},{4,5},{5,6},{6,7},{7,8},{8,9},{9,10},{10,1... | collective-permute-start | bytes 786440 | tf_op jit(solution)/shard_map/ppermute | solution.py:17
  9.1 13.9 %collective-permute-start.1 = (bf16[2,256,256]{2,1,0:T(8,128)(2,1)S(1)}, bf16[2,256,256]{2,1,0:T(8,128)(2,1)S(1)}, u32[]{:S(2)}, u32[]{:S(2)}) collective-permute-start(bf16[2,256,256]{2,1,0:T(8,128)(2,1)S(1)} %get-tuple-element.12), channel_id=1, source_target_pairs={{1,0},{2,1},{3,2},{4,3},{5,4},{6,5},{7,6},{8,7},{9,8},{10,9},{11,1... | collective-permute-start | bytes 786440 | tf_op jit(solution)/shard_map/ppermute | solution.py:18
  34.2 20.5 %all-to-all-start = ((f16[2,2,16,16,256]{4,3,0,1,2:T(8,128)(2,1)}), f16[2,2,16,16,256]{4,3,0,1,2:T(8,128)(2,1)S(1)}, u32[]{:S(2)}, u32[]{:S(2)}) async-start(f16[2,2,16,16,256]{4,3,0,1,2:T(8,128)(2,1)} %copy.8), calls=%async_computation | async-start | bytes 1048576 | tf_op jit(solution)/shard_map/all_to_all | solution.py:42
